TPU v7x, 256 devices: a whole 4x4x8 slice. The times are simulated.
256 devices in a mesh: sector: 64 (over z, y, core), dof: 4 (over x).
Axes of the slice: x: 4, y: 4, z: 8, core: 2. Of those that a mesh axis runs over, the one named last changes fastest.
Arguments:
- load_history: bfloat16 [64, 64, 6144], P('sector', None, 'dof'), may hold values from -6 to 6
- sector_basis: bfloat16 [6144, 1536], P('dof'), may hold values from -0.078125 to 0.078125
- harmonic_modes: bfloat16 [64, 1536, 256], P('sector'), may hold values from -0.15625 to 0.15625
- stress_basis: bfloat16 [1536, 6144], P(None, 'dof'), may hold values from -0.375 to 0.375
- mode_decay: float32 [64, 256], P('sector'), may hold values from 0.01 to 0.3
- mode_phase: float32 [64, 256], P('sector'), may hold values from 0.05 to 1.5
- mode_count: int32 [64], P('sector'), may hold values from 64 to 256, as said below
- slot_harmonic: int32 [64], replicated, may hold values from 0 to 63, each once
Outputs:
- stress_field: bfloat16 [64, 64, 6144], P('sector', None, 'dof')
Inputs may be any that keep to these rules, and one draw needn't show every extreme that they name: Slot modes from mode_count on are left out; some slot has 256 live modes and some 256 // 4. `slot_harmonic`: every harmonic component is held by exactly one slot.
All inputs are finite; a program needn't handle non-finite values.
Results may differ from a plain program's by a relative error of at most 0.025.
Values may be sent and summed in bfloat16 or wider, within the bound.
No kernel may reach another device: no remote copies, remote signals or barrier semaphores. Data moves between devices by JAX's collectives and lax.ppermute only.
A program may use at most 64 MiB of HBM per device.

v0:
```python
import math

import jax
import jax.numpy as jnp
from jax import lax
from jax.sharding import PartitionSpec as P


def transform_table(slot_harmonic):
    count_all = slot_harmonic.shape[0]
    half_count = count_all // 2
    sine_rows = slot_harmonic > half_count
    harmonic_order = jnp.where(sine_rows, slot_harmonic - half_count, slot_harmonic)
    sector_index = jnp.arange(count_all, dtype=jnp.int32)
    residue = harmonic_order[:, None] * sector_index[None, :] % count_all
    phase_angle = residue.astype(jnp.float32) * jnp.float32(2.0 * math.pi / count_all)
    wave_table = jnp.where(sine_rows[:, None], jnp.sin(phase_angle), jnp.cos(phase_angle))
    single = (slot_harmonic == 0) | (slot_harmonic == half_count)
    weight = jnp.where(single, jnp.float32(1.0 / count_all), jnp.float32(2.0 / count_all))
    return jnp.sqrt(weight)[:, None] * wave_table


def filter_kernel(decay_rates, phase_steps, steps_count):
    time_index = jnp.arange(steps_count, dtype=jnp.int32)
    offset = time_index[:, None] - time_index[None, :]
    causal = offset >= 0
    lag_value = jnp.maximum(offset, 0).astype(jnp.float32)
    gain_factor = jnp.sqrt(1.0 - jnp.exp(-2.0 * decay_rates))
    shape_table = (
        gain_factor[..., None, None]
        * jnp.exp(-decay_rates[..., None, None] * lag_value)
        * jnp.cos(phase_steps[..., None, None] * lag_value)
    )
    return jnp.where(causal, shape_table, jnp.float32(0.0))


def local(
    load_history,
    sector_basis,
    harmonic_modes,
    stress_basis,
    mode_decay,
    mode_phase,
    mode_count,
    slot_harmonic,
):
    highest = lax.Precision.HIGHEST
    table = transform_table(slot_harmonic)
    steps_count = load_history.shape[1]
    modes_slot = harmonic_modes[0]
    partial_value = jnp.dot(load_history[0], sector_basis, preferred_element_type=jnp.float32)
    live = (jnp.arange(modes_slot.shape[1], dtype=jnp.int32) < mode_count[0]).astype(jnp.float32)
    kernel = filter_kernel(mode_decay[0], mode_phase[0], steps_count)
    reduced = lax.psum(partial_value.astype(jnp.bfloat16), "dof")
    mixed = jnp.einsum(
        "ks,stc->ktc",
        table,
        lax.all_to_all(reduced[None], "sector", split_axis=1, concat_axis=0, tiled=True).astype(
            jnp.float32
        ),
        precision=highest,
    )
    spectrum = lax.all_to_all(
        mixed.astype(jnp.bfloat16), "sector", split_axis=0, concat_axis=1, tiled=True
    )[0]
    modal = jnp.dot(spectrum, modes_slot, preferred_element_type=jnp.float32) * live[None, :]
    response = jnp.einsum("mtu,um->tm", kernel, modal, precision=highest)
    project_response = response.astype(jnp.bfloat16)
    product = lax.dot_general(
        project_response, modes_slot, (((1,), (1,)), ((), ())), preferred_element_type=jnp.float32
    )
    returned = product.astype(jnp.bfloat16)
    mixed = jnp.einsum(
        "ks,ktc->stc",
        table,
        lax.all_to_all(returned[None], "sector", split_axis=1, concat_axis=0, tiled=True).astype(
            jnp.float32
        ),
        precision=highest,
    )
    back = lax.all_to_all(
        mixed.astype(jnp.bfloat16), "sector", split_axis=0, concat_axis=1, tiled=True
    )[0]
    stress_field = jnp.dot(back, stress_basis, preferred_element_type=jnp.float32).astype(
        jnp.bfloat16
    )
    return stress_field[None]


def solution(mesh):
    return jax.shard_map(
        local,
        mesh=mesh,
        in_specs=(
            P("sector", None, "dof"),
            P("dof", None),
            P("sector", None, None),
            P(None, "dof"),
            P("sector", None),
            P("sector", None),
            P("sector"),
            P(),
        ),
        out_specs=P("sector", None, "dof"),
        check_vma=False,
    )
```

profile of v0, /device:TPU:1, one launch (start us, length us, event | category | flops | bytes accessed | tf_op | source)
XLA Modules:
  0.0 171.5 jit_solution(9315487925137367451)
XLA Ops:
  6.5 4.1 %fusion.3 = bf16[1,64,1536]{2,1,0:T(8,128)(2,1)} fusion(bf16[1536,1536]{1,0:T(8,128)(2,1)} %param.9, bf16[1,64,1536]{2,1,0:T(8,128)(2,1)} %param.8), kind=kOutput, calls=%fused_computation.9 | convolution fusion | flops 302088192 | bytes 5111808 | tf_op jit(solution)/shard_map/dot_general | solution.py:51
  10.7 48.4 %all-reduce.2.cloned.1.call-done = bf16[1,64,1536]{2,1,0:T(8,128)(2,1)} async-done(((bf16[1,64,1536]{2,1,0:T(8,128)(2,1)}), bf16[1,64,1536]{2,1,0:T(8,128)(2,1)}) %all-reduce.2.cloned.1.call-update) | async-done | bytes 196624 | tf_op jit(solution)/shard_map/psum | solution.py:54
  59.1 1.2 copy.52
  60.3 0.6 broadcast.55
  60.9 1.8 %reduce.2 = bf16[64,1536]{1,0:T(8,128)(2,1)S(1)} reduce(bf16[64,1,1536]{2,1,0:T(2,128)(2,1)S(1)} %bitcast.50, bf16[]{:T(256)} %broadcast.55), dimensions={1}, to_apply=%bitcast.48.reduce_sub_computation | reduce | bytes 393218
  62.8 0.7 reshape.75
  63.5 12.8 %all-to-all-start = ((bf16[64,2,768]{2,1,0:T(2,128)(2,1)}), bf16[64,2,768]{2,1,0:T(2,128)(2,1)S(1)}, u32[]{:S(2)}, u32[]{:S(2)}) async-start(bf16[64,2,768]{2,1,0:T(2,128)(2,1)} %reshape.75), calls=%async_computation | async-start | bytes 393216 | tf_op jit(solution)/shard_map/all_to_all | solution.py:58
  77.0 11.3 %all-to-all-done = bf16[64,2,768]{2,1,0:T(2,128)(2,1)S(1)} async-done(((bf16[64,2,768]{2,1,0:T(2,128)(2,1)}), bf16[64,2,768]{2,1,0:T(2,128)(2,1)S(1)}, u32[]{:S(2)}, u32[]{:S(2)}) %all-to-all-start) | async-done | bytes 196640 | tf_op jit(solution)/shard_map/all_to_all | solution.py:58
  88.3 0.1 reshape.76
  88.5 0.5 fusion
  89.0 0.8 reduce.3
  89.8 0.7 reshape.77
  90.5 4.5 %all-to-all-start.1 = ((bf16[64,2,768]{2,1,0:T(2,128)(2,1)}), bf16[64,2,768]{2,1,0:T(2,128)(2,1)S(1)}, u32[]{:S(2)}, u32[]{:S(2)}) async-start(bf16[64,2,768]{2,1,0:T(2,128)(2,1)} %reshape.77), calls=%async_computation.1 | async-start | bytes 393216 | tf_op jit(solution)/shard_map/all_to_all | solution.py:63
  95.0 12.1 %all-to-all-done.1 = bf16[64,2,768]{2,1,0:T(2,128)(2,1)S(1)} async-done(((bf16[64,2,768]{2,1,0:T(2,128)(2,1)}), bf16[64,2,768]{2,1,0:T(2,128)(2,1)S(1)}, u32[]{:S(2)}, u32[]{:S(2)}) %all-to-all-start.1) | async-done | bytes 196640 | tf_op jit(solution)/shard_map/all_to_all | solution.py:63
  107.2 0.2 fusion.5
  107.5 16.2 %multiply_reduce_fusion = bf16[256,64]{0,1:T(8,128)(2,1)S(1)} fusion(f32[256,64]{0,1:T(8,128)S(1)} %fusion.5, f32[256]{0:T(256)S(1)} %bitcast.56, f32[64,64]{1,0:T(8,128)S(1)} %maximum_convert_fusion, f32[256]{0:T(256)S(1)} %bitcast.55, f32[256]{0:T(256)S(1)} %bitcast.54, pred[64,64]{1,0:T(8,128)(4,1)S(1)} %fusion.21), kind=kLoop, calls=%fused_computation | loop fusion | flops 7323648 | bytes 121856
  123.9 0.4 fusion.1
  124.2 0.3 copy.51
  124.6 1.8 %reduce.4 = bf16[64,1536]{1,0:T(8,128)(2,1)S(1)} reduce(bf16[64,1,1536]{2,1,0:T(2,128)(2,1)S(1)} %bitcast.51, bf16[]{:T(256)} %broadcast.55), dimensions={1}, to_apply=%bitcast.47.reduce_sub_computation | reduce | bytes 393218
  126.5 16.2 %all_to_all.16 = bf16[64,2,768]{2,1,0:T(2,128)(2,1)S(1)} all-to-all(bf16[64,2,768]{2,1,0:T(2,128)(2,1)S(1)} %reshape.79), channel_id=1, replica_groups=mesh['sector'=64,'dof'=4] {'sector'}, dimensions={0} | all-to-all | bytes 393216 | tf_op jit(solution)/shard_map/all_to_all | solution.py:76
  142.8 0.6 fusion.2
  143.4 0.8 reduce.5
  144.3 16.3 %all_to_all.17 = bf16[64,2,768]{2,1,0:T(2,128)(2,1)S(1)} all-to-all(bf16[64,2,768]{2,1,0:T(2,128)(2,1)S(1)} %reshape.81), channel_id=1, replica_groups=mesh['sector'=64,'dof'=4] {'sector'}, dimensions={0} | all-to-all | bytes 393216 | tf_op jit(solution)/shard_map/all_to_all | solution.py:81
  160.7 3.9 %fusion.4 = bf16[1,64,1536]{2,1,0:T(8,128)(2,1)} fusion(bf16[1536,1536]{1,0:T(8,128)(2,1)} %param.11, bf16[64,1,1536]{2,1,0:T(2,128)(2,1)S(1)} %reshape.82), kind=kOutput, calls=%fused_computation.10 | convolution fusion | flops 302088192 | bytes 5111808 | tf_op jit(solution)/shard_map/dot_general | solution.py:84
  (23 shorter events, 0.7 us)
Async XLA Ops:
  6.5 100.7 %copy-start = (bf16[1,1536,256]{2,1,0:T(8,128)(2,1)S(1)}, bf16[1,1536,256]{2,1,0:T(8,128)(2,1)}, u32[]{:S(2)}) copy-start(bf16[1,1536,256]{2,1,0:T(8,128)(2,1)} %param.10) | copy-start | bytes 2359300
  6.5 4.2 %copy-start.3 = (s32[64]{0:T(128)S(1)}, s32[64]{0:T(128)}, u32[]{:S(2)}) copy-start(s32[64]{0:T(128)} %param.15) | copy-start | bytes 772
  6.5 88.4 %copy-start.1 = (f32[1,256]{1,0:T(1,128)S(1)}, f32[1,256]{1,0:T(1,128)}, u32[]{:S(2)}) copy-start(f32[1,256]{1,0:T(1,128)} %param.12) | copy-start | bytes 3076
  6.5 52.5 %all-reduce.2.cloned.1.call-start = ((), (), s32[]{:S(2)}) async-start(), calls=%async_computation.4 | async-start | bytes 393216 | tf_op jit(solution)/shard_map/psum | solution.py:54
  10.7 96.8 %copy-start.2 = (f32[1,256]{1,0:T(1,128)S(1)}, f32[1,256]{1,0:T(1,128)}, u32[]{:S(2)}) copy-start(f32[1,256]{1,0:T(1,128)} %param.13) | copy-start | bytes 3076
  63.5 24.8 %all-to-all-start = ((bf16[64,2,768]{2,1,0:T(2,128)(2,1)}), bf16[64,2,768]{2,1,0:T(2,128)(2,1)S(1)}, u32[]{:S(2)}, u32[]{:S(2)}) async-start(bf16[64,2,768]{2,1,0:T(2,128)(2,1)} %reshape.75), calls=%async_computation | async-start | bytes 393216 | tf_op jit(solution)/shard_map/all_to_all | solution.py:58
  90.5 16.6 %all-to-all-start.1 = ((bf16[64,2,768]{2,1,0:T(2,128)(2,1)}), bf16[64,2,768]{2,1,0:T(2,128)(2,1)S(1)}, u32[]{:S(2)}, u32[]{:S(2)}) async-start(bf16[64,2,768]{2,1,0:T(2,128)(2,1)} %reshape.77), calls=%async_computation.1 | async-start | bytes 393216 | tf_op jit(solution)/shard_map/all_to_all | solution.py:63
Sparse Core Ops, SparseCore 0:
  10.8 48.2 all-reduce.1
where the time goes:
time: 172 us; the launch traced here: 171 us
  waiting for transfers between devices  71.8 us (42%)
  blocking collectives  32.5 us (19%)
  other arithmetic  21.5 us (12%)
  starting transfers between devices  17.3 us (10%)
  between operations  14.2 us (8%)
  matrix products  9.72 us (6%)
  local copies, waits for them, and re-layouts  4.4 us (3%)
    psum x1, waiting for transfers between devices, local(): reduced = lax.psum(partial_value.astype(jnp.bfloat16), 'dof')  48.4 us
    unnamed x3, other arithmetic  19.9 us
    all_to_all x1, blocking collectives, local(): lax.all_to_all(mixed.astype(jnp.bfloat16), 'sector', split_axis=0, concat...  16.3 us
    all_to_all x1, blocking collectives, local(): lax.all_to_all(returned[None], 'sector', split_axis=1, concat_axis=0, til...  16.2 us
    all_to_all x1, starting transfers between devices, local(): lax.all_to_all(reduced[None], 'sector', split_axis=1, concat_axis=0, tile...  12.8 us
    all_to_all x1, waiting for transfers between devices, local(): lax.all_to_all(mixed.astype(jnp.bfloat16), 'sector', split_axis=0, concat...  12.1 us
    all_to_all x1, waiting for transfers between devices, local(): lax.all_to_all(reduced[None], 'sector', split_axis=1, concat_axis=0, tile...  11.3 us
    all_to_all x1, starting transfers between devices, local(): lax.all_to_all(mixed.astype(jnp.bfloat16), 'sector', split_axis=0, concat...  4.47 us
  transfers between devices with their start and end apart: 3, of which 3 were waited for; matrix products, arithmetic and copies ran while one was open for 0% of the time, Pallas kernels for 0%

commit v1 on v0

--- a/solution.py
+++ b/solution.py
@@ -20,18 +20,24 @@
     return jnp.sqrt(weight)[:, None] * wave_table
 
 
-def filter_kernel(decay_rates, phase_steps, steps_count):
-    time_index = jnp.arange(steps_count, dtype=jnp.int32)
-    offset = time_index[:, None] - time_index[None, :]
-    causal = offset >= 0
-    lag_value = jnp.maximum(offset, 0).astype(jnp.float32)
+def lag_kernel(decay_rates, phase_steps, steps_count):
+    lag_value = jnp.arange(steps_count, dtype=jnp.int32).astype(jnp.float32)
     gain_factor = jnp.sqrt(1.0 - jnp.exp(-2.0 * decay_rates))
-    shape_table = (
-        gain_factor[..., None, None]
-        * jnp.exp(-decay_rates[..., None, None] * lag_value)
-        * jnp.cos(phase_steps[..., None, None] * lag_value)
+    return (
+        gain_factor[:, None]
+        * jnp.exp(-decay_rates[:, None] * lag_value[None, :])
+        * jnp.cos(phase_steps[:, None] * lag_value[None, :])
     )
-    return jnp.where(causal, shape_table, jnp.float32(0.0))
+
+
+def causal_response(lags, modal):
+    steps_count = modal.shape[0]
+    padded = jnp.concatenate([jnp.zeros_like(modal), modal], axis=0)
+    total = jnp.zeros_like(modal)
+    for n in range(steps_count):
+        shifted = lax.slice_in_dim(padded, steps_count - n, 2 * steps_count - n, axis=0)
+        total = total + lags[:, n][None, :] * shifted
+    return total
 
 
 def local(
@@ -45,26 +51,30 @@
     slot_harmonic,
 ):
     highest = lax.Precision.HIGHEST
+    n_sector = lax.axis_size("sector")
+    n_dof = lax.axis_size("dof")
+    n_all = n_sector * n_dof
     table = transform_table(slot_harmonic)
     steps_count = load_history.shape[1]
+    reduced_count = sector_basis.shape[1]
+    piece = steps_count * reduced_count // n_all
     modes_slot = harmonic_modes[0]
+
     partial_value = jnp.dot(load_history[0], sector_basis, preferred_element_type=jnp.float32)
+    sent = partial_value.astype(jnp.bfloat16).reshape(n_all, piece)
+    got = lax.all_to_all(sent, ("sector", "dof"), 0, 0, tiled=True)
+    reduced = got.reshape(n_sector, n_dof, piece).astype(jnp.float32).sum(axis=1)
+    reduced = reduced.astype(jnp.bfloat16).astype(jnp.float32)
+    mixed = jnp.dot(table, reduced, precision=highest).astype(jnp.bfloat16)
+    sent = jnp.repeat(mixed, n_dof, axis=0)
+    spectrum = lax.all_to_all(sent, ("sector", "dof"), 0, 0, tiled=True).reshape(
+        steps_count, reduced_count
+    )
+
     live = (jnp.arange(modes_slot.shape[1], dtype=jnp.int32) < mode_count[0]).astype(jnp.float32)
-    kernel = filter_kernel(mode_decay[0], mode_phase[0], steps_count)
-    reduced = lax.psum(partial_value.astype(jnp.bfloat16), "dof")
-    mixed = jnp.einsum(
-        "ks,stc->ktc",
-        table,
-        lax.all_to_all(reduced[None], "sector", split_axis=1, concat_axis=0, tiled=True).astype(
-            jnp.float32
-        ),
-        precision=highest,
-    )
-    spectrum = lax.all_to_all(
-        mixed.astype(jnp.bfloat16), "sector", split_axis=0, concat_axis=1, tiled=True
-    )[0]
     modal = jnp.dot(spectrum, modes_slot, preferred_element_type=jnp.float32) * live[None, :]
-    response = jnp.einsum("mtu,um->tm", kernel, modal, precision=highest)
+    lags = lag_kernel(mode_decay[0], mode_phase[0], steps_count)
+    response = causal_response(lags, modal)
     project_response = response.astype(jnp.bfloat16)
     product = lax.dot_general(
         project_response, modes_slot, (((1,), (1,)), ((), ())), preferred_element_type=jnp.float32

time: 172 us -> 107 us (0.62)
  waiting for transfers between devices: 71.8 us -> 29.4 us
  between operations: 14.2 us -> 0.94 us
  other arithmetic: 21.5 us -> 9.04 us
  starting transfers between devices: 17.3 us -> 21.2 us
    psum x1 -> x0, waiting for transfers between devices: 48.4 us -> none  [local(): reduced = lax.psum(partial_value.astype(jnp.bfloat16), 'dof')]
    unnamed x3 -> x1, other arithmetic: 19.9 us -> 1.79 us
    all_to_all x2, waiting for transfers between devices: 23.4 us -> 29.4 us  [the longest x1 14.8 us: local(): got = lax.all_to_all(sent, ('sector', 'dof'), 0, 0, tiled=True)]
    all_to_all x0 -> x4, other arithmetic: none -> 5.93 us  [the longest x2 2.97 us: local(): lax.all_to_all(sent, ('sector', 'dof'), 0, 0, tiled=True)]
    all_to_all x2, starting transfers between devices: 17.3 us -> 21.2 us  [the longest x1 15.7 us: local(): got = lax.all_to_all(sent, ('sector', 'dof'), 0, 0, tiled=True)]
  transfers between devices with their start and end apart: 3 -> 2, of which waited for: 3 -> 2; matrix products, arithmetic and copies ran while one was open for 0% -> 0% of each run, Pallas kernels for 0% -> 0%
where the time goes in v1:
time: 107 us
  blocking collectives  32.9 us (31%)
  waiting for transfers between devices  29.4 us (27%)
  starting transfers between devices  21.2 us (20%)
  matrix products  9.32 us (9%)
  other arithmetic  9.04 us (8%)
  local copies, waits for them, and re-layouts  4.09 us (4%)
    all_to_all x1, blocking collectives, local(): lax.all_to_all(returned[None], 'sector', split_axis=1, concat_axis=0, til...  16.6 us
    all_to_all x1, blocking collectives, local(): lax.all_to_all(mixed.astype(jnp.bfloat16), 'sector', split_axis=0, concat...  16.3 us
    all_to_all x1, starting transfers between devices, local(): got = lax.all_to_all(sent, ('sector', 'dof'), 0, 0, tiled=True)  15.7 us
    all_to_all x1, waiting for transfers between devices, local(): got = lax.all_to_all(sent, ('sector', 'dof'), 0, 0, tiled=True)  14.8 us
    all_to_all x1, waiting for transfers between devices, local(): lax.all_to_all(sent, ('sector', 'dof'), 0, 0, tiled=True)  14.6 us
    all_to_all x1, starting transfers between devices, local(): lax.all_to_all(sent, ('sector', 'dof'), 0, 0, tiled=True)  5.51 us
    dot_general x1, matrix products, local(): jnp.dot(back, stress_basis, preferred_element_type=jnp.float32)  3.91 us
    dot_general x1, matrix products, local(): jnp.dot(load_history[0], sector_basis, preferred_element_type=jnp.float32)  3.43 us
  transfers between devices with their start and end apart: 2, of which 2 were waited for; matrix products, arithmetic and copies ran while one was open for 0% of the time, Pallas kernels for 0%

profile of v1, /device:TPU:1, one launch (start us, length us, event | category | flops | bytes accessed | tf_op | source)
XLA Modules:
  0.0 106.8 jit_solution(12922636983058121031)
XLA Ops:
  0.0 3.4 %convolution_convert_fusion.3 = bf16[64,1536]{1,0:T(8,128)(2,1)S(1)} fusion(bf16[1536,1536]{1,0:T(8,128)(2,1)} %param.9, bf16[1,64,1536]{2,1,0:T(8,128)(2,1)} %param.8), kind=kOutput, calls=%fused_computation.3 | convolution fusion | flops 302088192 | bytes 5111808 | tf_op jit(solution)/shard_map/dot_general | solution.py:63
  3.6 0.5 broadcast.46
  4.1 1.8 %reduce.3 = bf16[256,384]{1,0:T(8,128)(2,1)S(1)} reduce(bf16[256,1,384]{2,1,0:T(2,128)(2,1)S(1)} %all_to_all.32, bf16[]{:T(256)} %broadcast.46), dimensions={1}, to_apply=%all_to_all.32.reduce_sub_computation | reduce | bytes 393218 | tf_op jit(solution)/shard_map/all_to_all | solution.py:65
  5.9 0.9 reshape.133
  6.8 15.7 %all-to-all-start = ((bf16[256,2,192]{2,1,0:T(2,128)(2,1)}), bf16[256,2,192]{2,1,0:T(2,128)(2,1)S(1)}, u32[]{:S(2)}, u32[]{:S(2)}) async-start(bf16[256,2,192]{2,1,0:T(2,128)(2,1)} %reshape.133), calls=%async_computation | async-start | bytes 524288 | tf_op jit(solution)/shard_map/all_to_all | solution.py:65
  22.5 0.3 cosine_multiply_fusion
  22.9 14.8 %all-to-all-done = bf16[256,2,192]{2,1,0:T(2,128)(2,1)S(1)} async-done(((bf16[256,2,192]{2,1,0:T(2,128)(2,1)}), bf16[256,2,192]{2,1,0:T(2,128)(2,1)S(1)}, u32[]{:S(2)}, u32[]{:S(2)}) %all-to-all-start) | async-done | bytes 196640 | tf_op jit(solution)/shard_map/all_to_all | solution.py:65
  37.7 0.3 reshape.134
  38.0 1.2 %reduce.1 = bf16[256,384]{1,0:T(8,128)(2,1)S(1)} reduce(bf16[256,1,384]{2,1,0:T(2,128)(2,1)S(1)} %reshape.134, bf16[]{:T(256)} %constant.42), dimensions={1}, to_apply=%all_to_all.27.reduce_sub_computation | reduce | bytes 393218 | tf_op jit(solution)/shard_map/all_to_all | solution.py:65
  39.5 0.4 convolution_convert_fusion.4
  40.0 1.8 %reduce.4 = bf16[256,384]{1,0:T(8,128)(2,1)S(1)} reduce(bf16[256,1,384]{2,1,0:T(2,128)(2,1)S(1)} %all_to_all.33, bf16[]{:T(256)} %broadcast.46), dimensions={1}, to_apply=%all_to_all.33.reduce_sub_computation | reduce | bytes 393218 | tf_op jit(solution)/shard_map/all_to_all | solution.py:70
  41.8 0.9 reshape.135
  42.7 5.5 %all-to-all-start.1 = ((bf16[256,2,192]{2,1,0:T(2,128)(2,1)}), bf16[256,2,192]{2,1,0:T(2,128)(2,1)S(1)}, u32[]{:S(2)}, u32[]{:S(2)}) async-start(bf16[256,2,192]{2,1,0:T(2,128)(2,1)} %reshape.135), calls=%async_computation.1 | async-start | bytes 524288 | tf_op jit(solution)/shard_map/all_to_all | solution.py:70
  48.9 14.6 %all-to-all-done.1 = bf16[256,2,192]{2,1,0:T(2,128)(2,1)S(1)} async-done(((bf16[256,2,192]{2,1,0:T(2,128)(2,1)}), bf16[256,2,192]{2,1,0:T(2,128)(2,1)S(1)}, u32[]{:S(2)}, u32[]{:S(2)}) %all-to-all-start.1) | async-done | bytes 196640 | tf_op jit(solution)/shard_map/all_to_all | solution.py:70
  63.5 0.3 reshape.136
  63.8 1.2 %reduce.2 = bf16[256,384]{1,0:T(8,128)(2,1)S(1)} reduce(bf16[256,1,384]{2,1,0:T(2,128)(2,1)S(1)} %reshape.136, bf16[]{:T(256)} %constant.42), dimensions={1}, to_apply=%all_to_all.29.reduce_sub_computation | reduce | bytes 393218 | tf_op jit(solution)/shard_map/all_to_all | solution.py:70
  65.4 0.8 fusion
  66.2 0.3 copy.28
  66.5 1.8 %reduce.5 = bf16[64,1536]{1,0:T(8,128)(2,1)S(1)} reduce(bf16[64,1,1536]{2,1,0:T(2,128)(2,1)S(1)} %bitcast.97, bf16[]{:T(256)} %broadcast.46), dimensions={1}, to_apply=%bitcast.95.reduce_sub_computation | reduce | bytes 393218
  68.3 16.6 %all_to_all.38 = bf16[64,2,768]{2,1,0:T(2,128)(2,1)S(1)} all-to-all(bf16[64,2,768]{2,1,0:T(2,128)(2,1)S(1)} %reshape.137), channel_id=1, replica_groups=mesh['sector'=64,'dof'=4] {'sector'}, dimensions={0} | all-to-all | bytes 393216 | tf_op jit(solution)/shard_map/all_to_all | solution.py:86
  85.1 0.6 fusion.1
  85.6 0.7 reduce.6
  86.4 16.3 %all_to_all.39 = bf16[64,2,768]{2,1,0:T(2,128)(2,1)S(1)} all-to-all(bf16[64,2,768]{2,1,0:T(2,128)(2,1)S(1)} %reshape.139), channel_id=1, replica_groups=mesh['sector'=64,'dof'=4] {'sector'}, dimensions={0} | all-to-all | bytes 393216 | tf_op jit(solution)/shard_map/all_to_all | solution.py:91
  102.9 3.9 %fusion.2 = bf16[1,64,1536]{2,1,0:T(8,128)(2,1)} fusion(bf16[1536,1536]{1,0:T(8,128)(2,1)} %param.11, bf16[64,1,1536]{2,1,0:T(2,128)(2,1)S(1)} %reshape.140), kind=kOutput, calls=%fused_computation.6 | convolution fusion | flops 302088192 | bytes 5111808 | tf_op jit(solution)/shard_map/dot_general | solution.py:94
  (29 shorter events, 1.4 us)
Async XLA Ops:
  0.0 65.1 %copy-start = (bf16[1,1536,256]{2,1,0:T(8,128)(2,1)S(1)}, bf16[1,1536,256]{2,1,0:T(8,128)(2,1)}, u32[]{:S(2)}) copy-start(bf16[1,1536,256]{2,1,0:T(8,128)(2,1)} %param.10) | copy-start | bytes 2359300
  0.0 22.4 %copy-start.3 = (s32[64]{0:T(128)S(1)}, s32[64]{0:T(128)}, u32[]{:S(2)}) copy-start(s32[64]{0:T(128)} %param.15) | copy-start | bytes 772
  0.0 22.5 %copy-start.2 = (f32[1,256]{1,0:T(1,128)S(1)}, f32[1,256]{1,0:T(1,128)}, u32[]{:S(2)}) copy-start(f32[1,256]{1,0:T(1,128)} %param.12) | copy-start | bytes 3076
  0.0 22.5 %copy-start.1 = (f32[1,256]{1,0:T(1,128)S(1)}, f32[1,256]{1,0:T(1,128)}, u32[]{:S(2)}) copy-start(f32[1,256]{1,0:T(1,128)} %param.13) | copy-start | bytes 3076
  6.8 30.9 %all-to-all-start = ((bf16[256,2,192]{2,1,0:T(2,128)(2,1)}), bf16[256,2,192]{2,1,0:T(2,128)(2,1)S(1)}, u32[]{:S(2)}, u32[]{:S(2)}) async-start(bf16[256,2,192]{2,1,0:T(2,128)(2,1)} %reshape.133), calls=%async_computation | async-start | bytes 524288 | tf_op jit(solution)/shard_map/all_to_all | solution.py:65
  42.7 20.8 %all-to-all-start.1 = ((bf16[256,2,192]{2,1,0:T(2,128)(2,1)}), bf16[256,2,192]{2,1,0:T(2,128)(2,1)S(1)}, u32[]{:S(2)}, u32[]{:S(2)}) async-start(bf16[256,2,192]{2,1,0:T(2,128)(2,1)} %reshape.135), calls=%async_computation.1 | async-start | bytes 524288 | tf_op jit(solution)/shard_map/all_to_all | solution.py:70

commit v2 on v1

--- a/solution.py
+++ b/solution.py
@@ -61,9 +61,9 @@
     modes_slot = harmonic_modes[0]
 
     partial_value = jnp.dot(load_history[0], sector_basis, preferred_element_type=jnp.float32)
-    sent = partial_value.astype(jnp.bfloat16).reshape(n_all, piece)
+    sent = partial_value.reshape(n_all, piece)
     got = lax.all_to_all(sent, ("sector", "dof"), 0, 0, tiled=True)
-    reduced = got.reshape(n_sector, n_dof, piece).astype(jnp.float32).sum(axis=1)
+    reduced = got.reshape(n_sector, n_dof, piece).sum(axis=1)
     reduced = reduced.astype(jnp.bfloat16).astype(jnp.float32)
     mixed = jnp.dot(table, reduced, precision=highest).astype(jnp.bfloat16)
     sent = jnp.repeat(mixed, n_dof, axis=0)
@@ -80,17 +80,9 @@
         project_response, modes_slot, (((1,), (1,)), ((), ())), preferred_element_type=jnp.float32
     )
     returned = product.astype(jnp.bfloat16)
-    mixed = jnp.einsum(
-        "ks,ktc->stc",
-        table,
-        lax.all_to_all(returned[None], "sector", split_axis=1, concat_axis=0, tiled=True).astype(
-            jnp.float32
-        ),
-        precision=highest,
-    )
-    back = lax.all_to_all(
-        mixed.astype(jnp.bfloat16), "sector", split_axis=0, concat_axis=1, tiled=True
-    )[0]
+    by_step = lax.all_to_all(returned, "sector", 0, 0, tiled=True).astype(jnp.float32)
+    mixed = jnp.dot(table.T, by_step, precision=highest).astype(jnp.bfloat16)
+    back = lax.all_to_all(mixed, "sector", 0, 0, tiled=True)
     stress_field = jnp.dot(back, stress_basis, preferred_element_type=jnp.float32).astype(
         jnp.bfloat16
     )

time: 107 us -> 106 us (level)
  other arithmetic: 9.04 us -> 5.94 us
  waiting for transfers between devices: 29.4 us -> 31.2 us
    all_to_all x2 -> x1, other arithmetic: 2.96 us -> 0.93 us  [local(): got = lax.all_to_all(sent, ('sector', 'dof'), 0, 0, tiled=True)]
    all_to_all x1, waiting for transfers between devices: 14.8 us -> 16.7 us  [local(): got = lax.all_to_all(sent, ('sector', 'dof'), 0, 0, tiled=True)]
    unnamed x1 -> x0, other arithmetic: 1.79 us -> none
    all_to_all x0 -> x2, other arithmetic: none -> 1.47 us  [the longest x1 0.74 us: local(): lax.all_to_all(returned, 'sector', 0, 0, tiled=True).astype(jnp.float32)]
    unnamed x16 -> x14, local copies, waits for them, and re-layouts: 2.79 us -> 1.6 us
where the time goes in v2:
time: 106 us
  blocking collectives  32.8 us (31%)
  waiting for transfers between devices  31.2 us (29%)
  starting transfers between devices  22.1 us (21%)
  matrix products  9.32 us (9%)
  other arithmetic  5.94 us (6%)
  local copies, waits for them, and re-layouts  3.77 us (4%)
    all_to_all x1, waiting for transfers between devices, local(): got = lax.all_to_all(sent, ('sector', 'dof'), 0, 0, tiled=True)  16.7 us
    all_to_all x1, blocking collectives, local(): lax.all_to_all(returned, 'sector', 0, 0, tiled=True).astype(jnp.float32)  16.5 us
    all_to_all x1, blocking collectives, local(): back = lax.all_to_all(mixed, 'sector', 0, 0, tiled=True)  16.3 us
    all_to_all x1, starting transfers between devices, local(): got = lax.all_to_all(sent, ('sector', 'dof'), 0, 0, tiled=True)  15.7 us
    all_to_all x1, waiting for transfers between devices, local(): lax.all_to_all(sent, ('sector', 'dof'), 0, 0, tiled=True)  14.5 us
    all_to_all x1, starting transfers between devices, local(): lax.all_to_all(sent, ('sector', 'dof'), 0, 0, tiled=True)  6.4 us
    dot_general x1, matrix products, local(): jnp.dot(back, stress_basis, preferred_element_type=jnp.float32)  3.92 us
    dot_general x1, matrix products, local(): jnp.dot(load_history[0], sector_basis, preferred_element_type=jnp.float32)  3.43 us
  transfers between devices with their start and end apart: 2, of which 2 were waited for; matrix products, arithmetic and copies ran while one was open for 0% of the time, Pallas kernels for 0%

profile of v2, /device:TPU:1, one launch (start us, length us, event | category | flops | bytes accessed | tf_op | source)
XLA Modules:
  0.0 106.0 jit_solution(4011321615085757249)
XLA Ops:
  0.0 3.4 %fusion.9 = f32[64,1536]{1,0:T(8,128)S(1)} fusion(bf16[1536,1536]{1,0:T(8,128)(2,1)} %param.9, bf16[1,64,1536]{2,1,0:T(8,128)(2,1)} %param.8), kind=kOutput, calls=%fused_computation.77 | convolution fusion | flops 301989888 | bytes 5308416 | tf_op jit(solution)/shard_map/dot_general | solution.py:63
  3.5 1.2 %all_to_all.38 = f32[256,1,384]{2,1,0:T(1,128)} reshape(f32[64,1536]{1,0:T(8,128)S(1)} %fusion.9) | data formatting | bytes 786432 | tf_op jit(solution)/shard_map/all_to_all | solution.py:65
  4.7 15.7 %all-to-all-start = ((f32[256,1,384]{2,1,0:T(1,128)}), f32[256,1,384]{2,1,0:T(1,128)S(1)}, u32[]{:S(2)}, u32[]{:S(2)}) async-start(f32[256,1,384]{2,1,0:T(1,128)} %all_to_all.38), calls=%async_computation | async-start | bytes 786432 | tf_op jit(solution)/shard_map/all_to_all | solution.py:65
  20.4 0.3 cosine_multiply_fusion
  20.8 16.7 %all-to-all-done = f32[256,1,384]{2,1,0:T(1,128)S(1)} async-done(((f32[256,1,384]{2,1,0:T(1,128)}), f32[256,1,384]{2,1,0:T(1,128)S(1)}, u32[]{:S(2)}, u32[]{:S(2)}) %all-to-all-start) | async-done | bytes 393248 | tf_op jit(solution)/shard_map/all_to_all | solution.py:65
  37.5 0.9 reduce
  38.5 0.2 reduce_sum.9
  38.8 0.4 convolution_convert_fusion.3
  39.3 0.5 broadcast.46
  39.8 1.8 %reduce.2 = bf16[256,384]{1,0:T(8,128)(2,1)S(1)} reduce(bf16[256,1,384]{2,1,0:T(2,128)(2,1)S(1)} %all_to_all.39, bf16[]{:T(256)} %broadcast.46), dimensions={1}, to_apply=%all_to_all.39.reduce_sub_computation | reduce | bytes 393218 | tf_op jit(solution)/shard_map/all_to_all | solution.py:70
  41.6 0.9 reshape.123
  42.5 6.4 %all-to-all-start.1 = ((bf16[256,2,192]{2,1,0:T(2,128)(2,1)}), bf16[256,2,192]{2,1,0:T(2,128)(2,1)S(1)}, u32[]{:S(2)}, u32[]{:S(2)}) async-start(bf16[256,2,192]{2,1,0:T(2,128)(2,1)} %reshape.123), calls=%async_computation.1 | async-start | bytes 524288 | tf_op jit(solution)/shard_map/all_to_all | solution.py:70
  49.6 14.5 %all-to-all-done.1 = bf16[256,2,192]{2,1,0:T(2,128)(2,1)S(1)} async-done(((bf16[256,2,192]{2,1,0:T(2,128)(2,1)}), bf16[256,2,192]{2,1,0:T(2,128)(2,1)S(1)}, u32[]{:S(2)}, u32[]{:S(2)}) %all-to-all-start.1) | async-done | bytes 196640 | tf_op jit(solution)/shard_map/all_to_all | solution.py:70
  64.2 0.3 reshape.124
  64.5 1.2 %reduce.1 = bf16[256,384]{1,0:T(8,128)(2,1)S(1)} reduce(bf16[256,1,384]{2,1,0:T(2,128)(2,1)S(1)} %reshape.124, bf16[]{:T(256)} %constant.41), dimensions={1}, to_apply=%all_to_all.31.reduce_sub_computation | reduce | bytes 393218 | tf_op jit(solution)/shard_map/all_to_all | solution.py:70
  65.8 0.3 convolution_multiply_fusion
  66.1 0.8 fusion
  66.8 0.7 reduce.3
  67.6 16.5 %all_to_all.44 = bf16[64,2,768]{2,1,0:T(2,128)(2,1)S(1)} all-to-all(bf16[64,2,768]{2,1,0:T(2,128)(2,1)S(1)} %reshape.125), channel_id=1, replica_groups=mesh['sector'=64,'dof'=4] {'sector'}, dimensions={0} | all-to-all | bytes 393216 | tf_op jit(solution)/shard_map/all_to_all | solution.py:83
  84.3 0.6 fusion.1
  84.9 0.7 reduce.4
  85.7 16.3 %all_to_all.45 = bf16[64,2,768]{2,1,0:T(2,128)(2,1)S(1)} all-to-all(bf16[64,2,768]{2,1,0:T(2,128)(2,1)S(1)} %reshape.127), channel_id=1, replica_groups=mesh['sector'=64,'dof'=4] {'sector'}, dimensions={0} | all-to-all | bytes 393216 | tf_op jit(solution)/shard_map/all_to_all | solution.py:85
  102.0 0.1 reshape.128
  102.1 3.9 %fusion.2 = bf16[1,64,1536]{2,1,0:T(8,128)(2,1)} fusion(bf16[1536,1536]{1,0:T(8,128)(2,1)} %param.11, bf16[64,1,1536]{2,1,0:T(2,128)(2,1)S(1)} %reshape.128), kind=kOutput, calls=%fused_computation.5 | convolution fusion | flops 302088192 | bytes 5111808 | tf_op jit(solution)/shard_map/dot_general | solution.py:86
  (25 shorter events, 0.8 us)
Async XLA Ops:
  0.0 65.8 %copy-start = (bf16[1,1536,256]{2,1,0:T(8,128)(2,1)S(1)}, bf16[1,1536,256]{2,1,0:T(8,128)(2,1)}, u32[]{:S(2)}) copy-start(bf16[1,1536,256]{2,1,0:T(8,128)(2,1)} %param.10) | copy-start | bytes 2359300
  0.0 20.3 %copy-start.3 = (s32[64]{0:T(128)S(1)}, s32[64]{0:T(128)}, u32[]{:S(2)}) copy-start(s32[64]{0:T(128)} %param.15) | copy-start | bytes 772
  0.0 20.4 %copy-start.2 = (f32[1,256]{1,0:T(1,128)S(1)}, f32[1,256]{1,0:T(1,128)}, u32[]{:S(2)}) copy-start(f32[1,256]{1,0:T(1,128)} %param.12) | copy-start | bytes 3076
  0.0 20.4 %copy-start.1 = (f32[1,256]{1,0:T(1,128)S(1)}, f32[1,256]{1,0:T(1,128)}, u32[]{:S(2)}) copy-start(f32[1,256]{1,0:T(1,128)} %param.13) | copy-start | bytes 3076
  4.7 32.8 %all-to-all-start = ((f32[256,1,384]{2,1,0:T(1,128)}), f32[256,1,384]{2,1,0:T(1,128)S(1)}, u32[]{:S(2)}, u32[]{:S(2)}) async-start(f32[256,1,384]{2,1,0:T(1,128)} %all_to_all.38), calls=%async_computation | async-start | bytes 786432 | tf_op jit(solution)/shard_map/all_to_all | solution.py:65
  42.5 21.7 %all-to-all-start.1 = ((bf16[256,2,192]{2,1,0:T(2,128)(2,1)}), bf16[256,2,192]{2,1,0:T(2,128)(2,1)S(1)}, u32[]{:S(2)}, u32[]{:S(2)}) async-start(bf16[256,2,192]{2,1,0:T(2,128)(2,1)} %reshape.123), calls=%async_computation.1 | async-start | bytes 524288 | tf_op jit(solution)/shard_map/all_to_all | solution.py:70

commit v3 on v2

--- a/solution.py
+++ b/solution.py
@@ -65,14 +65,15 @@
     got = lax.all_to_all(sent, ("sector", "dof"), 0, 0, tiled=True)
     reduced = got.reshape(n_sector, n_dof, piece).sum(axis=1)
     reduced = reduced.astype(jnp.bfloat16).astype(jnp.float32)
-    mixed = jnp.dot(table, reduced, precision=highest).astype(jnp.bfloat16)
-    sent = jnp.repeat(mixed, n_dof, axis=0)
+    sent = jnp.dot(jnp.repeat(table, n_dof, axis=0), reduced, precision=highest)
     spectrum = lax.all_to_all(sent, ("sector", "dof"), 0, 0, tiled=True).reshape(
         steps_count, reduced_count
     )
 
     live = (jnp.arange(modes_slot.shape[1], dtype=jnp.int32) < mode_count[0]).astype(jnp.float32)
-    modal = jnp.dot(spectrum, modes_slot, preferred_element_type=jnp.float32) * live[None, :]
+    modal = jnp.dot(
+        spectrum, modes_slot.astype(jnp.float32), precision=highest
+    ) * live[None, :]
     lags = lag_kernel(mode_decay[0], mode_phase[0], steps_count)
     response = causal_response(lags, modal)
     project_response = response.astype(jnp.bfloat16)

time: 106 us -> 107 us (level)
  other arithmetic: 5.94 us -> 4.11 us
  waiting for transfers between devices: 31.2 us -> 32.9 us
    all_to_all x1, waiting for transfers between devices: 14.5 us -> 17 us  [local(): lax.all_to_all(sent, ('sector', 'dof'), 0, 0, tiled=True)]
    all_to_all x2 -> x1, other arithmetic: 2.96 us -> 0.93 us  [local(): lax.all_to_all(sent, ('sector', 'dof'), 0, 0, tiled=True)]
    unnamed x14 -> x12, local copies, waits for them, and re-layouts: 1.6 us -> 0.41 us
  transfers between devices with their start and end apart: 2 -> 2, of which waited for: 2 -> 2; matrix products, arithmetic and copies ran while one was open for 0% -> 1% of each run, Pallas kernels for 0% -> 0%
where the time goes in v3:
time: 107 us
  blocking collectives  33.7 us (31%)
  waiting for transfers between devices  32.9 us (31%)
  starting transfers between devices  22.1 us (21%)
  matrix products  9.48 us (9%)
  other arithmetic  4.11 us (4%)
  local copies, waits for them, and re-layouts  3.54 us (3%)
    all_to_all x1, blocking collectives, local(): lax.all_to_all(returned, 'sector', 0, 0, tiled=True).astype(jnp.float32)  17.4 us
    all_to_all x1, waiting for transfers between devices, local(): lax.all_to_all(sent, ('sector', 'dof'), 0, 0, tiled=True)  17 us
    all_to_all x1, blocking collectives, local(): back = lax.all_to_all(mixed, 'sector', 0, 0, tiled=True)  16.3 us
    all_to_all x1, waiting for transfers between devices, local(): got = lax.all_to_all(sent, ('sector', 'dof'), 0, 0, tiled=True)  15.8 us
    all_to_all x1, starting transfers between devices, local(): got = lax.all_to_all(sent, ('sector', 'dof'), 0, 0, tiled=True)  15.7 us
    all_to_all x1, starting transfers between devices, local(): lax.all_to_all(sent, ('sector', 'dof'), 0, 0, tiled=True)  6.41 us
    dot_general x1, matrix products, local(): jnp.dot(back, stress_basis, preferred_element_type=jnp.float32)  3.92 us
    dot_general x1, matrix products, local(): jnp.dot(load_history[0], sector_basis, preferred_element_type=jnp.float32)  3.43 us
  transfers between devices with their start and end apart: 2, of which 2 were waited for; matrix products, arithmetic and copies ran while one was open for 1% of the time, Pallas kernels for 0%

profile of v3, /device:TPU:1, one launch (start us, length us, event | category | flops | bytes accessed | tf_op | source)
XLA Modules:
  0.0 106.7 jit_solution(11958997198047128773)
XLA Ops:
  0.0 3.4 %fusion.9 = f32[64,1536]{1,0:T(8,128)S(1)} fusion(bf16[1536,1536]{1,0:T(8,128)(2,1)} %param.9, bf16[1,64,1536]{2,1,0:T(8,128)(2,1)} %param.8), kind=kOutput, calls=%fused_computation.77 | convolution fusion | flops 301989888 | bytes 5308416 | tf_op jit(solution)/shard_map/dot_general | solution.py:63
  3.5 1.2 %all_to_all.38 = f32[256,1,384]{2,1,0:T(1,128)} reshape(f32[64,1536]{1,0:T(8,128)S(1)} %fusion.9) | data formatting | bytes 786432 | tf_op jit(solution)/shard_map/all_to_all | solution.py:65
  4.7 15.7 %all-to-all-start = ((f32[256,1,384]{2,1,0:T(1,128)}), f32[256,1,384]{2,1,0:T(1,128)S(1)}, u32[]{:S(2)}, u32[]{:S(2)}) async-start(f32[256,1,384]{2,1,0:T(1,128)} %all_to_all.38), calls=%async_computation | async-start | bytes 786432 | tf_op jit(solution)/shard_map/all_to_all | solution.py:65
  21.1 0.3 cosine_multiply_fusion
  21.4 0.2 select_multiply_fusion
  21.6 15.8 %all-to-all-done = f32[256,1,384]{2,1,0:T(1,128)S(1)} async-done(((f32[256,1,384]{2,1,0:T(1,128)}), f32[256,1,384]{2,1,0:T(1,128)S(1)}, u32[]{:S(2)}, u32[]{:S(2)}) %all-to-all-start) | async-done | bytes 393248 | tf_op jit(solution)/shard_map/all_to_all | solution.py:65
  37.5 0.9 reduce
  38.5 0.2 reduce_sum.9
  38.8 0.3 convolution_bitcast_fusion
  39.1 1.1 %copy.14 = f32[256,1,384]{2,1,0:T(1,128)} copy(f32[256,1,384]{2,0,1:T(8,128)S(1)} %convolution_bitcast_fusion) | data formatting | bytes 786432 | tf_op jit(solution)/shard_map/all_to_all | solution.py:69
  40.2 6.4 %all-to-all-start.1 = ((f32[256,1,384]{2,1,0:T(1,128)}), f32[256,1,384]{2,1,0:T(1,128)S(1)}, u32[]{:S(2)}, u32[]{:S(2)}) async-start(f32[256,1,384]{2,1,0:T(1,128)} %copy.14), calls=%async_computation.1 | async-start | bytes 786432 | tf_op jit(solution)/shard_map/all_to_all | solution.py:69
  46.7 17.0 %all-to-all-done.1 = f32[256,1,384]{2,1,0:T(1,128)S(1)} async-done(((f32[256,1,384]{2,1,0:T(1,128)}), f32[256,1,384]{2,1,0:T(1,128)S(1)}, u32[]{:S(2)}, u32[]{:S(2)}) %all-to-all-start.1) | async-done | bytes 393248 | tf_op jit(solution)/shard_map/all_to_all | solution.py:69
  63.8 0.9 reduce.1
  64.8 0.5 convolution_multiply_fusion
  65.3 0.8 fusion
  66.1 0.5 broadcast.45
  66.6 0.7 reduce.2
  67.4 17.4 %all_to_all.43 = bf16[64,2,768]{2,1,0:T(2,128)(2,1)S(1)} all-to-all(bf16[64,2,768]{2,1,0:T(2,128)(2,1)S(1)} %reshape.125), channel_id=1, replica_groups=mesh['sector'=64,'dof'=4] {'sector'}, dimensions={0} | all-to-all | bytes 393216 | tf_op jit(solution)/shard_map/all_to_all | solution.py:84
  84.8 0.1 reshape.126
  84.9 0.6 fusion.1
  85.5 0.7 reduce.3
  86.3 16.3 %all_to_all.44 = bf16[64,2,768]{2,1,0:T(2,128)(2,1)S(1)} all-to-all(bf16[64,2,768]{2,1,0:T(2,128)(2,1)S(1)} %reshape.127), channel_id=1, replica_groups=mesh['sector'=64,'dof'=4] {'sector'}, dimensions={0} | all-to-all | bytes 393216 | tf_op jit(solution)/shard_map/all_to_all | solution.py:86
  102.6 0.1 reshape.128
  102.7 3.9 %fusion.2 = bf16[1,64,1536]{2,1,0:T(8,128)(2,1)} fusion(bf16[1536,1536]{1,0:T(8,128)(2,1)} %param.11, bf16[64,1,1536]{2,1,0:T(2,128)(2,1)S(1)} %reshape.128), kind=kOutput, calls=%fused_computation.5 | convolution fusion | flops 302088192 | bytes 5111808 | tf_op jit(solution)/shard_map/dot_general | solution.py:87
  (23 shorter events, 0.4 us)
Async XLA Ops:
  0.0 64.8 %copy-start = (bf16[1,1536,256]{2,1,0:T(8,128)(2,1)S(1)}, bf16[1,1536,256]{2,1,0:T(8,128)(2,1)}, u32[]{:S(2)}) copy-start(bf16[1,1536,256]{2,1,0:T(8,128)(2,1)} %param.10) | copy-start | bytes 2359300
  0.0 20.3 %copy-start.3 = (s32[64]{0:T(128)S(1)}, s32[64]{0:T(128)}, u32[]{:S(2)}) copy-start(s32[64]{0:T(128)} %param.15) | copy-start | bytes 772
  0.0 21.0 %copy-start.2 = (f32[1,256]{1,0:T(1,128)S(1)}, f32[1,256]{1,0:T(1,128)}, u32[]{:S(2)}) copy-start(f32[1,256]{1,0:T(1,128)} %param.12) | copy-start | bytes 3076
  0.0 21.1 %copy-start.1 = (f32[1,256]{1,0:T(1,128)S(1)}, f32[1,256]{1,0:T(1,128)}, u32[]{:S(2)}) copy-start(f32[1,256]{1,0:T(1,128)} %param.13) | copy-start | bytes 3076
  4.7 32.8 %all-to-all-start = ((f32[256,1,384]{2,1,0:T(1,128)}), f32[256,1,384]{2,1,0:T(1,128)S(1)}, u32[]{:S(2)}, u32[]{:S(2)}) async-start(f32[256,1,384]{2,1,0:T(1,128)} %all_to_all.38), calls=%async_computation | async-start | bytes 786432 | tf_op jit(solution)/shard_map/all_to_all | solution.py:65
  40.2 23.6 %all-to-all-start.1 = ((f32[256,1,384]{2,1,0:T(1,128)}), f32[256,1,384]{2,1,0:T(1,128)S(1)}, u32[]{:S(2)}, u32[]{:S(2)}) async-start(f32[256,1,384]{2,1,0:T(1,128)} %copy.14), calls=%async_computation.1 | async-start | bytes 786432 | tf_op jit(solution)/shard_map/all_to_all | solution.py:69

commit v4 on v3

--- a/solution.py
+++ b/solution.py
@@ -63,9 +63,8 @@
     partial_value = jnp.dot(load_history[0], sector_basis, preferred_element_type=jnp.float32)
     sent = partial_value.reshape(n_all, piece)
     got = lax.all_to_all(sent, ("sector", "dof"), 0, 0, tiled=True)
-    reduced = got.reshape(n_sector, n_dof, piece).sum(axis=1)
-    reduced = reduced.astype(jnp.bfloat16).astype(jnp.float32)
-    sent = jnp.dot(jnp.repeat(table, n_dof, axis=0), reduced, precision=highest)
+    wide_table = jnp.repeat(jnp.repeat(table, n_dof, axis=0), n_dof, axis=1)
+    sent = jnp.dot(wide_table, got, precision=highest)
     spectrum = lax.all_to_all(sent, ("sector", "dof"), 0, 0, tiled=True).reshape(
         steps_count, reduced_count
     )

time: 107 us -> 106 us (level)
  other arithmetic: 4.11 us -> 2.94 us
where the time goes in v4:
time: 106 us
  blocking collectives  33.7 us (32%)
  waiting for transfers between devices  32.6 us (31%)
  starting transfers between devices  22.1 us (21%)
  matrix products  9.81 us (9%)
  local copies, waits for them, and re-layouts  3.66 us (3%)
  other arithmetic  2.94 us (3%)
    all_to_all x1, blocking collectives, local(): lax.all_to_all(returned, 'sector', 0, 0, tiled=True).astype(jnp.float32)  17.4 us
    all_to_all x1, waiting for transfers between devices, local(): lax.all_to_all(sent, ('sector', 'dof'), 0, 0, tiled=True)  17 us
    all_to_all x1, blocking collectives, local(): back = lax.all_to_all(mixed, 'sector', 0, 0, tiled=True)  16.3 us
    all_to_all x1, starting transfers between devices, local(): got = lax.all_to_all(sent, ('sector', 'dof'), 0, 0, tiled=True)  15.7 us
    all_to_all x1, waiting for transfers between devices, local(): got = lax.all_to_all(sent, ('sector', 'dof'), 0, 0, tiled=True)  15.6 us
    all_to_all x1, starting transfers between devices, local(): lax.all_to_all(sent, ('sector', 'dof'), 0, 0, tiled=True)  6.4 us
    dot_general x1, matrix products, local(): jnp.dot(back, stress_basis, preferred_element_type=jnp.float32)  3.92 us
    dot_general x1, matrix products, local(): jnp.dot(load_history[0], sector_basis, preferred_element_type=jnp.float32)  3.43 us
  transfers between devices with their start and end apart: 2, of which 2 were waited for; matrix products, arithmetic and copies ran while one was open for 1% of the time, Pallas kernels for 0%

profile of v4, /device:TPU:1, one launch (start us, length us, event | category | flops | bytes accessed | tf_op | source)
XLA Modules:
  0.0 105.7 jit_solution(6663185296608950859)
XLA Ops:
  0.0 3.4 %fusion.11 = f32[64,1536]{1,0:T(8,128)S(1)} fusion(bf16[1536,1536]{1,0:T(8,128)(2,1)} %param.9, bf16[1,64,1536]{2,1,0:T(8,128)(2,1)} %param.8), kind=kOutput, calls=%fused_computation.79 | convolution fusion | flops 301989888 | bytes 5308416 | tf_op jit(solution)/shard_map/dot_general | solution.py:63
  3.5 1.2 %all_to_all.41 = f32[256,1,384]{2,1,0:T(1,128)} reshape(f32[64,1536]{1,0:T(8,128)S(1)} %fusion.11) | data formatting | bytes 786432 | tf_op jit(solution)/shard_map/all_to_all | solution.py:65
  4.7 15.7 %all-to-all-start = ((f32[256,1,384]{2,1,0:T(1,128)}), f32[256,1,384]{2,1,0:T(1,128)S(1)}, u32[]{:S(2)}, u32[]{:S(2)}) async-start(f32[256,1,384]{2,1,0:T(1,128)} %all_to_all.41), calls=%async_computation | async-start | bytes 786432 | tf_op jit(solution)/shard_map/all_to_all | solution.py:65
  20.4 0.2 select_multiply_fusion
  20.6 0.1 copy.15
  20.8 0.1 reshape.120
  21.6 0.3 cosine_multiply_fusion
  21.9 15.6 %all-to-all-done = f32[256,1,384]{2,1,0:T(1,128)S(1)} async-done(((f32[256,1,384]{2,1,0:T(1,128)}), f32[256,1,384]{2,1,0:T(1,128)S(1)}, u32[]{:S(2)}, u32[]{:S(2)}) %all-to-all-start) | async-done | bytes 393248 | tf_op jit(solution)/shard_map/all_to_all | solution.py:65
  37.5 0.6 convolution_bitcast_fusion
  38.1 1.2 %copy.17 = f32[256,1,384]{2,1,0:T(1,128)} copy(f32[256,1,384]{2,0,1:T(8,128)S(1)} %convolution_bitcast_fusion) | data formatting | bytes 786432 | tf_op jit(solution)/shard_map/all_to_all | solution.py:68
  39.2 6.4 %all-to-all-start.1 = ((f32[256,1,384]{2,1,0:T(1,128)}), f32[256,1,384]{2,1,0:T(1,128)S(1)}, u32[]{:S(2)}, u32[]{:S(2)}) async-start(f32[256,1,384]{2,1,0:T(1,128)} %copy.17), calls=%async_computation.1 | async-start | bytes 786432 | tf_op jit(solution)/shard_map/all_to_all | solution.py:68
  45.8 17.0 %all-to-all-done.1 = f32[256,1,384]{2,1,0:T(1,128)S(1)} async-done(((f32[256,1,384]{2,1,0:T(1,128)}), f32[256,1,384]{2,1,0:T(1,128)S(1)}, u32[]{:S(2)}, u32[]{:S(2)}) %all-to-all-start.1) | async-done | bytes 393248 | tf_op jit(solution)/shard_map/all_to_all | solution.py:68
  62.8 0.9 reduce
  63.8 0.5 convolution_multiply_fusion
  64.3 0.8 fusion
  65.1 0.5 broadcast.44
  65.6 0.7 reduce.1
  66.4 17.4 %all_to_all.46 = bf16[64,2,768]{2,1,0:T(2,128)(2,1)S(1)} all-to-all(bf16[64,2,768]{2,1,0:T(2,128)(2,1)S(1)} %reshape.123), channel_id=1, replica_groups=mesh['sector'=64,'dof'=4] {'sector'}, dimensions={0} | all-to-all | bytes 393216 | tf_op jit(solution)/shard_map/all_to_all | solution.py:83
  83.8 0.1 reshape.124
  83.9 0.6 fusion.1
  84.5 0.7 reduce.2
  85.3 16.3 %all_to_all.47 = bf16[64,2,768]{2,1,0:T(2,128)(2,1)S(1)} all-to-all(bf16[64,2,768]{2,1,0:T(2,128)(2,1)S(1)} %reshape.125), channel_id=1, replica_groups=mesh['sector'=64,'dof'=4] {'sector'}, dimensions={0} | all-to-all | bytes 393216 | tf_op jit(solution)/shard_map/all_to_all | solution.py:85
  101.6 0.1 reshape.126
  101.7 3.9 %fusion.2 = bf16[1,64,1536]{2,1,0:T(8,128)(2,1)} fusion(bf16[1536,1536]{1,0:T(8,128)(2,1)} %param.11, bf16[64,1,1536]{2,1,0:T(2,128)(2,1)S(1)} %reshape.126), kind=kOutput, calls=%fused_computation.5 | convolution fusion | flops 302088192 | bytes 5111808 | tf_op jit(solution)/shard_map/dot_general | solution.py:86
  (23 shorter events, 0.4 us)
Async XLA Ops:
  0.0 63.8 %copy-start = (bf16[1,1536,256]{2,1,0:T(8,128)(2,1)S(1)}, bf16[1,1536,256]{2,1,0:T(8,128)(2,1)}, u32[]{:S(2)}) copy-start(bf16[1,1536,256]{2,1,0:T(8,128)(2,1)} %param.10) | copy-start | bytes 2359300
  0.0 20.3 %copy-start.3 = (s32[64]{0:T(128)S(1)}, s32[64]{0:T(128)}, u32[]{:S(2)}) copy-start(s32[64]{0:T(128)} %param.15) | copy-start | bytes 772
  0.0 21.5 %copy-start.2 = (f32[1,256]{1,0:T(1,128)S(1)}, f32[1,256]{1,0:T(1,128)}, u32[]{:S(2)}) copy-start(f32[1,256]{1,0:T(1,128)} %param.12) | copy-start | bytes 3076
  0.0 21.6 %copy-start.1 = (f32[1,256]{1,0:T(1,128)S(1)}, f32[1,256]{1,0:T(1,128)}, u32[]{:S(2)}) copy-start(f32[1,256]{1,0:T(1,128)} %param.13) | copy-start | bytes 3076
  4.7 32.8 %all-to-all-start = ((f32[256,1,384]{2,1,0:T(1,128)}), f32[256,1,384]{2,1,0:T(1,128)S(1)}, u32[]{:S(2)}, u32[]{:S(2)}) async-start(f32[256,1,384]{2,1,0:T(1,128)} %all_to_all.41), calls=%async_computation | async-start | bytes 786432 | tf_op jit(solution)/shard_map/all_to_all | solution.py:65
  39.2 23.5 %all-to-all-start.1 = ((f32[256,1,384]{2,1,0:T(1,128)}), f32[256,1,384]{2,1,0:T(1,128)S(1)}, u32[]{:S(2)}, u32[]{:S(2)}) async-start(f32[256,1,384]{2,1,0:T(1,128)} %copy.17), calls=%async_computation.1 | async-start | bytes 786432 | tf_op jit(solution)/shard_map/all_to_all | solution.py:68

commit v5 on v4

--- a/solution.py
+++ b/solution.py
@@ -61,8 +61,8 @@
     modes_slot = harmonic_modes[0]
 
     partial_value = jnp.dot(load_history[0], sector_basis, preferred_element_type=jnp.float32)
-    sent = partial_value.reshape(n_all, piece)
-    got = lax.all_to_all(sent, ("sector", "dof"), 0, 0, tiled=True)
+    sent = partial_value.reshape(n_all, 1, piece)
+    got = lax.all_to_all(sent, ("sector", "dof"), 0, 0, tiled=True).reshape(n_all, piece)
     wide_table = jnp.repeat(jnp.repeat(table, n_dof, axis=0), n_dof, axis=1)
     sent = jnp.dot(wide_table, got, precision=highest)
     spectrum = lax.all_to_all(sent, ("sector", "dof"), 0, 0, tiled=True).reshape(
@@ -80,12 +80,16 @@
         project_response, modes_slot, (((1,), (1,)), ((), ())), preferred_element_type=jnp.float32
     )
     returned = product.astype(jnp.bfloat16)
-    by_step = lax.all_to_all(returned, "sector", 0, 0, tiled=True).astype(jnp.float32)
-    mixed = jnp.dot(table.T, by_step, precision=highest).astype(jnp.bfloat16)
+    halves = (n_sector, 2, reduced_count // 2)
+    by_step = lax.all_to_all(returned.reshape(halves), "sector", 0, 0, tiled=True)
+    mixed = jnp.einsum(
+        "js,jhc->shc", table, by_step.astype(jnp.float32), precision=highest
+    ).astype(jnp.bfloat16)
     back = lax.all_to_all(mixed, "sector", 0, 0, tiled=True)
-    stress_field = jnp.dot(back, stress_basis, preferred_element_type=jnp.float32).astype(
-        jnp.bfloat16
-    )
+    stress_field = jnp.einsum(
+        "thc,hcn->tn", back, stress_basis.reshape(halves[1], halves[2], -1),
+        preferred_element_type=jnp.float32,
+    ).astype(jnp.bfloat16)
     return stress_field[None]
 
 

time: 106 us -> 104 us (0.981)
  other arithmetic: 2.94 us -> 1.42 us
    all_to_all x1 -> x2, starting transfers between devices: 6.4 us -> 22.1 us  [local(): lax.all_to_all(sent, ('sector', 'dof'), 0, 0, tiled=True)]
    all_to_all x1 -> x0, starting transfers between devices: 15.7 us -> none  [local(): got = lax.all_to_all(sent, ('sector', 'dof'), 0, 0, tiled=True)]
    all_to_all x1 -> x0, waiting for transfers between devices: 15.6 us -> none  [local(): got = lax.all_to_all(sent, ('sector', 'dof'), 0, 0, tiled=True)]
    all_to_all x1 -> x2, waiting for transfers between devices: 17 us -> 32.6 us  [local(): lax.all_to_all(sent, ('sector', 'dof'), 0, 0, tiled=True)]
    all_to_all x2 -> x0, local copies, waits for them, and re-layouts: 1.72 us -> none  [the longest x1 1.21 us: local(): got = lax.all_to_all(sent, ('sector', 'dof'), 0, 0, tiled=True)]
    all_to_all x2 -> x0, other arithmetic: 1.46 us -> none  [the longest x1 0.73 us: local(): back = lax.all_to_all(mixed, 'sector', 0, 0, tiled=True)]
    reshape x0 -> x2, local copies, waits for them, and re-layouts: none -> 1.26 us  [the longest x1 1.21 us: local(): sent = partial_value.reshape(n_all, 1, piece)]
where the time goes in v5:
time: 104 us; the launch traced here: 103 us
  blocking collectives  33.7 us (32%)
  waiting for transfers between devices  32.6 us (31%)
  starting transfers between devices  22.1 us (21%)
  matrix products  9.69 us (9%)
  local copies, waits for them, and re-layouts  3.08 us (3%)
  other arithmetic  1.42 us (1%)
    all_to_all x2, waiting for transfers between devices, local(): lax.all_to_all(sent, ('sector', 'dof'), 0, 0, tiled=True)  32.6 us
    all_to_all x2, starting transfers between devices, local(): lax.all_to_all(sent, ('sector', 'dof'), 0, 0, tiled=True)  22.1 us
    all_to_all x1, blocking collectives, local(): lax.all_to_all(returned.reshape(halves), 'sector', 0, 0, tiled=True)  17.4 us
    all_to_all x1, blocking collectives, local(): back = lax.all_to_all(mixed, 'sector', 0, 0, tiled=True)  16.3 us
    dot_general x1, matrix products, local(): jnp.einsum('thc,hcn->tn', back, stress_basis.reshape(halves[1], halves[2]...  3.91 us
    dot_general x1, matrix products, local(): jnp.dot(load_history[0], sector_basis, preferred_element_type=jnp.float32)  3.43 us
  transfers between devices with their start and end apart: 2, of which 2 were waited for; matrix products, arithmetic and copies ran while one was open for 1% of the time, Pallas kernels for 0%

profile of v5, /device:TPU:1, one launch (start us, length us, event | category | flops | bytes accessed | tf_op | source)
XLA Modules:
  0.0 103.4 jit_solution(10545221219576766582)
XLA Ops:
  0.0 0.0 copy-start
  0.0 3.4 %fusion.6 = f32[64,1536]{1,0:T(8,128)S(1)} fusion(bf16[1536,1536]{1,0:T(8,128)(2,1)} %param.9, bf16[1,64,1536]{2,1,0:T(8,128)(2,1)} %param.8), kind=kOutput, calls=%fused_computation.74 | convolution fusion | flops 301989888 | bytes 5308416 | tf_op jit(solution)/shard_map/dot_general | solution.py:63
  3.5 1.2 %reshape.132 = f32[256,1,384]{2,1,0:T(1,128)} reshape(f32[64,1536]{1,0:T(8,128)S(1)} %fusion.6) | data formatting | bytes 786432 | tf_op jit(solution)/shard_map/reshape | solution.py:64
  4.7 15.7 %all-to-all-start = ((f32[256,1,384]{2,1,0:T(1,128)}), f32[256,1,384]{2,1,0:T(1,128)S(1)}, u32[]{:S(2)}, u32[]{:S(2)}) async-start(f32[256,1,384]{2,1,0:T(1,128)} %reshape.132), calls=%async_computation | async-start | bytes 786432 | tf_op jit(solution)/shard_map/all_to_all | solution.py:65
  20.4 0.2 select_multiply_fusion
  20.5 0.1 copy.12
  20.7 0.1 copy.13
  20.8 0.1 reshape.124
  21.6 0.3 cosine_multiply_fusion
  21.9 15.6 %all-to-all-done = f32[256,1,384]{2,1,0:T(1,128)S(1)} async-done(((f32[256,1,384]{2,1,0:T(1,128)}), f32[256,1,384]{2,1,0:T(1,128)S(1)}, u32[]{:S(2)}, u32[]{:S(2)}) %all-to-all-start) | async-done | bytes 393248 | tf_op jit(solution)/shard_map/all_to_all | solution.py:65
  37.5 0.6 convolution_bitcast_fusion.1
  38.1 1.2 %copy.15 = f32[256,1,384]{2,1,0:T(1,128)} copy(f32[256,1,384]{2,0,1:T(8,128)S(1)} %convolution_bitcast_fusion.1) | data formatting | bytes 786432 | tf_op jit(solution)/shard_map/all_to_all | solution.py:68
  39.2 6.4 %all-to-all-start.1 = ((f32[256,1,384]{2,1,0:T(1,128)}), f32[256,1,384]{2,1,0:T(1,128)S(1)}, u32[]{:S(2)}, u32[]{:S(2)}) async-start(f32[256,1,384]{2,1,0:T(1,128)} %copy.15), calls=%async_computation.1 | async-start | bytes 786432 | tf_op jit(solution)/shard_map/all_to_all | solution.py:68
  45.8 17.0 %all-to-all-done.1 = f32[256,1,384]{2,1,0:T(1,128)S(1)} async-done(((f32[256,1,384]{2,1,0:T(1,128)}), f32[256,1,384]{2,1,0:T(1,128)S(1)}, u32[]{:S(2)}, u32[]{:S(2)}) %all-to-all-start.1) | async-done | bytes 393248 | tf_op jit(solution)/shard_map/all_to_all | solution.py:68
  62.8 0.9 reduce
  63.7 0.1 reshape.127
  63.8 0.5 convolution_multiply_fusion
  64.3 0.8 convolution_convert_fusion
  65.1 0.1 reshape.128
  65.2 17.4 %all_to_all.24 = bf16[64,2,768]{2,1,0:T(2,128)(2,1)S(1)} all-to-all(bf16[64,2,768]{2,1,0:T(2,128)(2,1)S(1)} %reshape.128), channel_id=1, replica_groups=mesh['sector'=64,'dof'=4] {'sector'}, dimensions={0} | all-to-all | bytes 393216 | tf_op jit(solution)/shard_map/all_to_all | solution.py:84
  82.5 0.5 convolution_convert_fusion.1
  83.0 0.2 copy.17
  83.2 16.3 %all_to_all.25 = bf16[64,2,768]{2,1,0:T(2,128)(2,1)S(1)} all-to-all(bf16[64,2,768]{2,1,0:T(2,128)(2,1)S(1)} %copy.17), channel_id=1, replica_groups=mesh['sector'=64,'dof'=4] {'sector'}, dimensions={0} | all-to-all | bytes 393216 | tf_op jit(solution)/shard_map/all_to_all | solution.py:88
  99.5 3.9 %fusion.1 = bf16[1,64,1536]{2,1,0:T(8,128)(2,1)} fusion(bf16[2,768,1536]{2,1,0:T(8,128)(2,1)} %bitcast.101, bf16[64,2,768]{2,1,0:T(2,128)(2,1)S(1)} %all_to_all.25), kind=kOutput, calls=%fused_computation.3 | convolution fusion | flops 302088192 | bytes 5111808 | tf_op jit(solution)/shard_map/thc,hcn->tn/dot_general | solution.py:89
  (19 shorter events, 0.2 us)
Async XLA Ops:
  0.0 63.8 %copy-start = (bf16[1,1536,256]{2,1,0:T(8,128)(2,1)S(1)}, bf16[1,1536,256]{2,1,0:T(8,128)(2,1)}, u32[]{:S(2)}) copy-start(bf16[1,1536,256]{2,1,0:T(8,128)(2,1)} %param.10) | copy-start | bytes 2359300
  0.0 20.3 %copy-start.3 = (s32[64]{0:T(128)S(1)}, s32[64]{0:T(128)}, u32[]{:S(2)}) copy-start(s32[64]{0:T(128)} %param.15) | copy-start | bytes 772
  0.0 21.5 %copy-start.2 = (f32[1,256]{1,0:T(1,128)S(1)}, f32[1,256]{1,0:T(1,128)}, u32[]{:S(2)}) copy-start(f32[1,256]{1,0:T(1,128)} %param.12) | copy-start | bytes 3076
  0.0 21.6 %copy-start.1 = (f32[1,256]{1,0:T(1,128)S(1)}, f32[1,256]{1,0:T(1,128)}, u32[]{:S(2)}) copy-start(f32[1,256]{1,0:T(1,128)} %param.13) | copy-start | bytes 3076
  4.7 32.8 %all-to-all-start = ((f32[256,1,384]{2,1,0:T(1,128)}), f32[256,1,384]{2,1,0:T(1,128)S(1)}, u32[]{:S(2)}, u32[]{:S(2)}) async-start(f32[256,1,384]{2,1,0:T(1,128)} %reshape.132), calls=%async_computation | async-start | bytes 786432 | tf_op jit(solution)/shard_map/all_to_all | solution.py:65
  39.2 23.6 %all-to-all-start.1 = ((f32[256,1,384]{2,1,0:T(1,128)}), f32[256,1,384]{2,1,0:T(1,128)S(1)}, u32[]{:S(2)}, u32[]{:S(2)}) async-start(f32[256,1,384]{2,1,0:T(1,128)} %copy.15), calls=%async_computation.1 | async-start | bytes 786432 | tf_op jit(solution)/shard_map/all_to_all | solution.py:68

commit v6 on v5

--- a/solution.py
+++ b/solution.py
@@ -64,15 +64,14 @@
     sent = partial_value.reshape(n_all, 1, piece)
     got = lax.all_to_all(sent, ("sector", "dof"), 0, 0, tiled=True).reshape(n_all, piece)
     wide_table = jnp.repeat(jnp.repeat(table, n_dof, axis=0), n_dof, axis=1)
-    sent = jnp.dot(wide_table, got, precision=highest)
+    sent = jnp.dot(wide_table, got, precision=highest).astype(jnp.bfloat16)
+    sent = sent.reshape(n_all, 2, piece // 2)
     spectrum = lax.all_to_all(sent, ("sector", "dof"), 0, 0, tiled=True).reshape(
         steps_count, reduced_count
     )
 
     live = (jnp.arange(modes_slot.shape[1], dtype=jnp.int32) < mode_count[0]).astype(jnp.float32)
-    modal = jnp.dot(
-        spectrum, modes_slot.astype(jnp.float32), precision=highest
-    ) * live[None, :]
+    modal = jnp.dot(spectrum, modes_slot, preferred_element_type=jnp.float32) * live[None, :]
     lags = lag_kernel(mode_decay[0], mode_phase[0], steps_count)
     response = causal_response(lags, modal)
     project_response = response.astype(jnp.bfloat16)

time: 104 us -> 99.8 us (0.960)
  waiting for transfers between devices: 32.6 us -> 30.7 us
    all_to_all x2, waiting for transfers between devices: 32.6 us -> 30.7 us  [local(): lax.all_to_all(sent, ('sector', 'dof'), 0, 0, tiled=True)]
    all_to_all x1 -> x0, local copies, waits for them, and re-layouts: 1.15 us -> none  [local(): lax.all_to_all(sent, ('sector', 'dof'), 0, 0, tiled=True)]
where the time goes in v6:
time: 99.8 us; the launch traced here: 99.5 us
  blocking collectives  32.9 us (33%)
  waiting for transfers between devices  30.7 us (31%)
  starting transfers between devices  22.1 us (22%)
  matrix products  9.43 us (9%)
  local copies, waits for them, and re-layouts  3.08 us (3%)
    all_to_all x2, waiting for transfers between devices, local(): lax.all_to_all(sent, ('sector', 'dof'), 0, 0, tiled=True)  30.7 us
    all_to_all x2, starting transfers between devices, local(): lax.all_to_all(sent, ('sector', 'dof'), 0, 0, tiled=True)  22.1 us
    all_to_all x1, blocking collectives, local(): lax.all_to_all(returned.reshape(halves), 'sector', 0, 0, tiled=True)  16.6 us
    all_to_all x1, blocking collectives, local(): back = lax.all_to_all(mixed, 'sector', 0, 0, tiled=True)  16.3 us
    dot_general x1, matrix products, local(): jnp.einsum('thc,hcn->tn', back, stress_basis.reshape(halves[1], halves[2]...  3.91 us
    dot_general x1, matrix products, local(): jnp.dot(load_history[0], sector_basis, preferred_element_type=jnp.float32)  3.43 us
  transfers between devices with their start and end apart: 2, of which 2 were waited for; matrix products, arithmetic and copies ran while one was open for 1% of the time, Pallas kernels for 0%

profile of v6, /device:TPU:1, one launch (start us, length us, event | category | flops | bytes accessed | tf_op | source)
XLA Modules:
  0.0 99.5 jit_solution(16589938115678210832)
XLA Ops:
  0.0 0.0 copy-start
  0.0 3.4 %fusion.6 = f32[64,1536]{1,0:T(8,128)S(1)} fusion(bf16[1536,1536]{1,0:T(8,128)(2,1)} %param.9, bf16[1,64,1536]{2,1,0:T(8,128)(2,1)} %param.8), kind=kOutput, calls=%fused_computation.74 | convolution fusion | flops 301989888 | bytes 5308416 | tf_op jit(solution)/shard_map/dot_general | solution.py:63
  3.5 1.2 %reshape.133 = f32[256,1,384]{2,1,0:T(1,128)} reshape(f32[64,1536]{1,0:T(8,128)S(1)} %fusion.6) | data formatting | bytes 786432 | tf_op jit(solution)/shard_map/reshape | solution.py:64
  4.7 15.7 %all-to-all-start = ((f32[256,1,384]{2,1,0:T(1,128)}), f32[256,1,384]{2,1,0:T(1,128)S(1)}, u32[]{:S(2)}, u32[]{:S(2)}) async-start(f32[256,1,384]{2,1,0:T(1,128)} %reshape.133), calls=%async_computation | async-start | bytes 786432 | tf_op jit(solution)/shard_map/all_to_all | solution.py:65
  20.4 0.2 select_multiply_fusion
  20.5 0.1 copy.16
  20.6 0.1 copy.17
  20.8 0.1 reshape.124
  20.9 0.3 cosine_multiply_fusion
  21.3 16.2 %all-to-all-done = f32[256,1,384]{2,1,0:T(1,128)S(1)} async-done(((f32[256,1,384]{2,1,0:T(1,128)}), f32[256,1,384]{2,1,0:T(1,128)S(1)}, u32[]{:S(2)}, u32[]{:S(2)}) %all-to-all-start) | async-done | bytes 393248 | tf_op jit(solution)/shard_map/all_to_all | solution.py:65
  37.5 0.6 convolution_convert_fusion.2
  38.1 0.1 copy.19
  38.2 0.9 copy.20
  39.1 6.4 %all-to-all-start.1 = ((bf16[256,2,192]{2,1,0:T(2,128)(2,1)}), bf16[256,2,192]{2,1,0:T(2,128)(2,1)S(1)}, u32[]{:S(2)}, u32[]{:S(2)}) async-start(bf16[256,2,192]{2,1,0:T(2,128)(2,1)} %copy.20), calls=%async_computation.1 | async-start | bytes 524288 | tf_op jit(solution)/shard_map/all_to_all | solution.py:69
  46.2 14.5 %all-to-all-done.1 = bf16[256,2,192]{2,1,0:T(2,128)(2,1)S(1)} async-done(((bf16[256,2,192]{2,1,0:T(2,128)(2,1)}), bf16[256,2,192]{2,1,0:T(2,128)(2,1)S(1)}, u32[]{:S(2)}, u32[]{:S(2)}) %all-to-all-start.1) | async-done | bytes 196640 | tf_op jit(solution)/shard_map/all_to_all | solution.py:69
  60.8 0.2 reshape.128
  61.0 0.3 convolution_multiply_fusion
  61.2 0.8 convolution_convert_fusion
  62.0 0.1 reshape.129
  62.1 16.6 %all_to_all.20 = bf16[64,2,768]{2,1,0:T(2,128)(2,1)S(1)} all-to-all(bf16[64,2,768]{2,1,0:T(2,128)(2,1)S(1)} %reshape.129), channel_id=1, replica_groups=mesh['sector'=64,'dof'=4] {'sector'}, dimensions={0} | all-to-all | bytes 393216 | tf_op jit(solution)/shard_map/all_to_all | solution.py:83
  78.6 0.5 convolution_convert_fusion.1
  79.1 0.2 copy.22
  79.3 16.3 %all_to_all.21 = bf16[64,2,768]{2,1,0:T(2,128)(2,1)S(1)} all-to-all(bf16[64,2,768]{2,1,0:T(2,128)(2,1)S(1)} %copy.22), channel_id=1, replica_groups=mesh['sector'=64,'dof'=4] {'sector'}, dimensions={0} | all-to-all | bytes 393216 | tf_op jit(solution)/shard_map/all_to_all | solution.py:87
  95.6 3.9 %fusion.1 = bf16[1,64,1536]{2,1,0:T(8,128)(2,1)} fusion(bf16[2,768,1536]{2,1,0:T(8,128)(2,1)} %bitcast.100, bf16[64,2,768]{2,1,0:T(2,128)(2,1)S(1)} %all_to_all.21), kind=kOutput, calls=%fused_computation.3 | convolution fusion | flops 302088192 | bytes 5111808 | tf_op jit(solution)/shard_map/thc,hcn->tn/dot_general | solution.py:88
  (19 shorter events, 0.2 us)
Async XLA Ops:
  0.0 61.0 %copy-start = (bf16[1,1536,256]{2,1,0:T(8,128)(2,1)S(1)}, bf16[1,1536,256]{2,1,0:T(8,128)(2,1)}, u32[]{:S(2)}) copy-start(bf16[1,1536,256]{2,1,0:T(8,128)(2,1)} %param.10) | copy-start | bytes 2359300
  0.0 20.3 %copy-start.3 = (s32[64]{0:T(128)S(1)}, s32[64]{0:T(128)}, u32[]{:S(2)}) copy-start(s32[64]{0:T(128)} %param.15) | copy-start | bytes 772
  0.0 20.9 %copy-start.2 = (f32[1,256]{1,0:T(1,128)S(1)}, f32[1,256]{1,0:T(1,128)}, u32[]{:S(2)}) copy-start(f32[1,256]{1,0:T(1,128)} %param.12) | copy-start | bytes 3076
  0.0 20.9 %copy-start.1 = (f32[1,256]{1,0:T(1,128)S(1)}, f32[1,256]{1,0:T(1,128)}, u32[]{:S(2)}) copy-start(f32[1,256]{1,0:T(1,128)} %param.13) | copy-start | bytes 3076
  4.7 32.8 %all-to-all-start = ((f32[256,1,384]{2,1,0:T(1,128)}), f32[256,1,384]{2,1,0:T(1,128)S(1)}, u32[]{:S(2)}, u32[]{:S(2)}) async-start(f32[256,1,384]{2,1,0:T(1,128)} %reshape.133), calls=%async_computation | async-start | bytes 786432 | tf_op jit(solution)/shard_map/all_to_all | solution.py:65
  39.1 21.6 %all-to-all-start.1 = ((bf16[256,2,192]{2,1,0:T(2,128)(2,1)}), bf16[256,2,192]{2,1,0:T(2,128)(2,1)S(1)}, u32[]{:S(2)}, u32[]{:S(2)}) async-start(bf16[256,2,192]{2,1,0:T(2,128)(2,1)} %copy.20), calls=%async_computation.1 | async-start | bytes 524288 | tf_op jit(solution)/shard_map/all_to_all | solution.py:69

commit v7 on v6

--- a/solution.py
+++ b/solution.py
@@ -61,10 +61,10 @@
     modes_slot = harmonic_modes[0]
 
     partial_value = jnp.dot(load_history[0], sector_basis, preferred_element_type=jnp.float32)
-    sent = partial_value.reshape(n_all, 1, piece)
+    sent = partial_value.astype(jnp.bfloat16).reshape(n_all, 2, piece // 2)
     got = lax.all_to_all(sent, ("sector", "dof"), 0, 0, tiled=True).reshape(n_all, piece)
     wide_table = jnp.repeat(jnp.repeat(table, n_dof, axis=0), n_dof, axis=1)
-    sent = jnp.dot(wide_table, got, precision=highest).astype(jnp.bfloat16)
+    sent = jnp.dot(wide_table, got.astype(jnp.float32), precision=highest).astype(jnp.bfloat16)
     sent = sent.reshape(n_all, 2, piece // 2)
     spectrum = lax.all_to_all(sent, ("sector", "dof"), 0, 0, tiled=True).reshape(
         steps_count, reduced_count

time: 99.8 us -> 96.9 us (0.971)
  waiting for transfers between devices: 30.7 us -> 28.8 us
    all_to_all x2, waiting for transfers between devices: 30.7 us -> 28.8 us  [local(): lax.all_to_all(sent, ('sector', 'dof'), 0, 0, tiled=True)]
where the time goes in v7:
time: 96.9 us; the launch traced here: 96.6 us
  blocking collectives  32.9 us (34%)
  waiting for transfers between devices  28.8 us (30%)
  starting transfers between devices  21.2 us (22%)
  matrix products  9.44 us (10%)
  local copies, waits for them, and re-layouts  3 us (3%)
    all_to_all x2, waiting for transfers between devices, local(): lax.all_to_all(sent, ('sector', 'dof'), 0, 0, tiled=True)  28.8 us
    all_to_all x2, starting transfers between devices, local(): lax.all_to_all(sent, ('sector', 'dof'), 0, 0, tiled=True)  21.2 us
    all_to_all x1, blocking collectives, local(): lax.all_to_all(returned.reshape(halves), 'sector', 0, 0, tiled=True)  16.6 us
    all_to_all x1, blocking collectives, local(): back = lax.all_to_all(mixed, 'sector', 0, 0, tiled=True)  16.3 us
    dot_general x1, matrix products, local(): jnp.einsum('thc,hcn->tn', back, stress_basis.reshape(halves[1], halves[2]...  3.91 us
    dot_general x1, matrix products, local(): jnp.dot(load_history[0], sector_basis, preferred_element_type=jnp.float32)  3.43 us
  transfers between devices with their start and end apart: 2, of which 2 were waited for; matrix products, arithmetic and copies ran while one was open for 1% of the time, Pallas kernels for 0%

profile of v7, /device:TPU:1, one launch (start us, length us, event | category | flops | bytes accessed | tf_op | source)
XLA Modules:
  0.0 96.6 jit_solution(6053082013660761449)
XLA Ops:
  0.0 3.4 %convolution_convert_fusion.1 = bf16[64,1536]{1,0:T(8,128)(2,1)S(1)} fusion(bf16[1536,1536]{1,0:T(8,128)(2,1)} %param.9, bf16[1,64,1536]{2,1,0:T(8,128)(2,1)} %param.8), kind=kOutput, calls=%fused_computation.3 | convolution fusion | flops 302088192 | bytes 5111808 | tf_op jit(solution)/shard_map/dot_general | solution.py:63
  3.5 1.0 reshape.125
  4.4 15.7 %all-to-all-start = ((bf16[256,2,192]{2,1,0:T(2,128)(2,1)}), bf16[256,2,192]{2,1,0:T(2,128)(2,1)S(1)}, u32[]{:S(2)}, u32[]{:S(2)}) async-start(bf16[256,2,192]{2,1,0:T(2,128)(2,1)} %reshape.125), calls=%async_computation | async-start | bytes 524288 | tf_op jit(solution)/shard_map/all_to_all | solution.py:65
  20.1 0.2 select_multiply_fusion
  20.3 0.1 copy.18
  20.4 0.1 copy.19
  20.5 0.1 reshape.124
  20.7 0.3 cosine_multiply_fusion
  21.0 14.3 %all-to-all-done = bf16[256,2,192]{2,1,0:T(2,128)(2,1)S(1)} async-done(((bf16[256,2,192]{2,1,0:T(2,128)(2,1)}), bf16[256,2,192]{2,1,0:T(2,128)(2,1)S(1)}, u32[]{:S(2)}, u32[]{:S(2)}) %all-to-all-start) | async-done | bytes 196640 | tf_op jit(solution)/shard_map/all_to_all | solution.py:65
  35.3 0.2 copy.20
  35.5 0.6 convolution_convert_fusion.3
  36.1 0.1 copy.21
  36.3 0.9 copy.22
  37.1 5.5 %all-to-all-start.1 = ((bf16[256,2,192]{2,1,0:T(2,128)(2,1)}), bf16[256,2,192]{2,1,0:T(2,128)(2,1)S(1)}, u32[]{:S(2)}, u32[]{:S(2)}) async-start(bf16[256,2,192]{2,1,0:T(2,128)(2,1)} %copy.22), calls=%async_computation.1 | async-start | bytes 524288 | tf_op jit(solution)/shard_map/all_to_all | solution.py:69
  43.4 14.5 %all-to-all-done.1 = bf16[256,2,192]{2,1,0:T(2,128)(2,1)S(1)} async-done(((bf16[256,2,192]{2,1,0:T(2,128)(2,1)}), bf16[256,2,192]{2,1,0:T(2,128)(2,1)S(1)}, u32[]{:S(2)}, u32[]{:S(2)}) %all-to-all-start.1) | async-done | bytes 196640 | tf_op jit(solution)/shard_map/all_to_all | solution.py:69
  57.9 0.2 reshape.128
  58.1 0.3 convolution_multiply_fusion
  58.4 0.8 convolution_convert_fusion
  59.1 0.1 reshape.129
  59.2 16.6 %all_to_all.20 = bf16[64,2,768]{2,1,0:T(2,128)(2,1)S(1)} all-to-all(bf16[64,2,768]{2,1,0:T(2,128)(2,1)S(1)} %reshape.129), channel_id=1, replica_groups=mesh['sector'=64,'dof'=4] {'sector'}, dimensions={0} | all-to-all | bytes 393216 | tf_op jit(solution)/shard_map/all_to_all | solution.py:83
  75.8 0.5 convolution_convert_fusion.2
  76.2 0.2 copy.24
  76.4 16.3 %all_to_all.21 = bf16[64,2,768]{2,1,0:T(2,128)(2,1)S(1)} all-to-all(bf16[64,2,768]{2,1,0:T(2,128)(2,1)S(1)} %copy.24), channel_id=1, replica_groups=mesh['sector'=64,'dof'=4] {'sector'}, dimensions={0} | all-to-all | bytes 393216 | tf_op jit(solution)/shard_map/all_to_all | solution.py:87
  92.7 3.9 %fusion.1 = bf16[1,64,1536]{2,1,0:T(8,128)(2,1)} fusion(bf16[2,768,1536]{2,1,0:T(8,128)(2,1)} %bitcast.99, bf16[64,2,768]{2,1,0:T(2,128)(2,1)S(1)} %all_to_all.21), kind=kOutput, calls=%fused_computation.4 | convolution fusion | flops 302088192 | bytes 5111808 | tf_op jit(solution)/shard_map/thc,hcn->tn/dot_general | solution.py:88
  (20 shorter events, 0.2 us)
Async XLA Ops:
  0.0 58.1 %copy-start = (bf16[1,1536,256]{2,1,0:T(8,128)(2,1)S(1)}, bf16[1,1536,256]{2,1,0:T(8,128)(2,1)}, u32[]{:S(2)}) copy-start(bf16[1,1536,256]{2,1,0:T(8,128)(2,1)} %param.10) | copy-start | bytes 2359300
  0.0 20.1 %copy-start.3 = (s32[64]{0:T(128)S(1)}, s32[64]{0:T(128)}, u32[]{:S(2)}) copy-start(s32[64]{0:T(128)} %param.15) | copy-start | bytes 772
  0.0 20.6 %copy-start.2 = (f32[1,256]{1,0:T(1,128)S(1)}, f32[1,256]{1,0:T(1,128)}, u32[]{:S(2)}) copy-start(f32[1,256]{1,0:T(1,128)} %param.12) | copy-start | bytes 3076
  0.0 20.7 %copy-start.1 = (f32[1,256]{1,0:T(1,128)S(1)}, f32[1,256]{1,0:T(1,128)}, u32[]{:S(2)}) copy-start(f32[1,256]{1,0:T(1,128)} %param.13) | copy-start | bytes 3076
  4.4 30.9 %all-to-all-start = ((bf16[256,2,192]{2,1,0:T(2,128)(2,1)}), bf16[256,2,192]{2,1,0:T(2,128)(2,1)S(1)}, u32[]{:S(2)}, u32[]{:S(2)}) async-start(bf16[256,2,192]{2,1,0:T(2,128)(2,1)} %reshape.125), calls=%async_computation | async-start | bytes 524288 | tf_op jit(solution)/shard_map/all_to_all | solution.py:65
  37.1 20.8 %all-to-all-start.1 = ((bf16[256,2,192]{2,1,0:T(2,128)(2,1)}), bf16[256,2,192]{2,1,0:T(2,128)(2,1)S(1)}, u32[]{:S(2)}, u32[]{:S(2)}) async-start(bf16[256,2,192]{2,1,0:T(2,128)(2,1)} %copy.22), calls=%async_computation.1 | async-start | bytes 524288 | tf_op jit(solution)/shard_map/all_to_all | solution.py:69

commit v8 on v7

--- a/solution.py
+++ b/solution.py
@@ -63,9 +63,11 @@
     partial_value = jnp.dot(load_history[0], sector_basis, preferred_element_type=jnp.float32)
     sent = partial_value.astype(jnp.bfloat16).reshape(n_all, 2, piece // 2)
     got = lax.all_to_all(sent, ("sector", "dof"), 0, 0, tiled=True).reshape(n_all, piece)
-    wide_table = jnp.repeat(jnp.repeat(table, n_dof, axis=0), n_dof, axis=1)
-    sent = jnp.dot(wide_table, got.astype(jnp.float32), precision=highest).astype(jnp.bfloat16)
-    sent = sent.reshape(n_all, 2, piece // 2)
+    wide_table = jnp.repeat(table, n_dof, axis=1)
+    mixed = jnp.dot(wide_table, got.astype(jnp.float32), precision=highest).astype(jnp.bfloat16)
+    sent = jnp.broadcast_to(
+        mixed.reshape(n_sector, 1, 2, piece // 2), (n_sector, n_dof, 2, piece // 2)
+    ).reshape(n_all, 2, piece // 2)
     spectrum = lax.all_to_all(sent, ("sector", "dof"), 0, 0, tiled=True).reshape(
         steps_count, reduced_count
     )

time: 96.9 us -> 96.6 us (level)
    reshape x3 -> x0, local copies, waits for them, and re-layouts: 1.04 us -> none  [the longest x1 0.87 us: local(): sent = sent.reshape(n_all, 2, piece // 2)]
where the time goes in v8:
time: 96.6 us; the launch traced here: 96.4 us
  blocking collectives  32.9 us (34%)
  waiting for transfers between devices  29.1 us (30%)
  starting transfers between devices  21.2 us (22%)
  matrix products  9.2 us (10%)
  local copies, waits for them, and re-layouts  2.63 us (3%)
    all_to_all x2, waiting for transfers between devices, local(): lax.all_to_all(sent, ('sector', 'dof'), 0, 0, tiled=True)  29.1 us
    all_to_all x2, starting transfers between devices, local(): lax.all_to_all(sent, ('sector', 'dof'), 0, 0, tiled=True)  21.2 us
    all_to_all x1, blocking collectives, local(): lax.all_to_all(returned.reshape(halves), 'sector', 0, 0, tiled=True)  16.6 us
    all_to_all x1, blocking collectives, local(): back = lax.all_to_all(mixed, 'sector', 0, 0, tiled=True)  16.3 us
    dot_general x1, matrix products, local(): jnp.einsum('thc,hcn->tn', back, stress_basis.reshape(halves[1], halves[2]...  3.91 us
    dot_general x1, matrix products, local(): jnp.dot(load_history[0], sector_basis, preferred_element_type=jnp.float32)  3.43 us
  transfers between devices with their start and end apart: 2, of which 2 were waited for; matrix products, arithmetic and copies ran while one was open for 1% of the time, Pallas kernels for 0%

profile of v8, /device:TPU:1, one launch (start us, length us, event | category | flops | bytes accessed | tf_op | source)
XLA Modules:
  0.0 96.4 jit_solution(13568393523903129768)
XLA Ops:
  0.0 0.0 copy-start
  0.0 0.0 copy-start.1
  0.0 3.4 %convolution_convert_fusion.1 = bf16[64,1536]{1,0:T(8,128)(2,1)S(1)} fusion(bf16[1536,1536]{1,0:T(8,128)(2,1)} %param.9, bf16[1,64,1536]{2,1,0:T(8,128)(2,1)} %param.8), kind=kOutput, calls=%fused_computation.3 | convolution fusion | flops 302088192 | bytes 5111808 | tf_op jit(solution)/shard_map/dot_general | solution.py:63
  3.5 1.0 reshape.123
  4.4 15.7 %all-to-all-start = ((bf16[256,2,192]{2,1,0:T(2,128)(2,1)}), bf16[256,2,192]{2,1,0:T(2,128)(2,1)S(1)}, u32[]{:S(2)}, u32[]{:S(2)}) async-start(bf16[256,2,192]{2,1,0:T(2,128)(2,1)} %reshape.123), calls=%async_computation | async-start | bytes 524288 | tf_op jit(solution)/shard_map/all_to_all | solution.py:65
  20.2 0.3 cosine_multiply_fusion
  20.5 0.2 select_multiply_fusion
  20.7 14.6 %all-to-all-done = bf16[256,2,192]{2,1,0:T(2,128)(2,1)S(1)} async-done(((bf16[256,2,192]{2,1,0:T(2,128)(2,1)}), bf16[256,2,192]{2,1,0:T(2,128)(2,1)S(1)}, u32[]{:S(2)}, u32[]{:S(2)}) %all-to-all-start) | async-done | bytes 196640 | tf_op jit(solution)/shard_map/all_to_all | solution.py:65
  35.3 0.2 copy.14
  35.5 0.4 convolution_convert_fusion.3
  35.9 0.1 broadcast_in_dim.42
  36.0 0.8 broadcast_in_dim.43
  36.9 5.5 %all-to-all-start.1 = ((bf16[256,2,192]{2,1,0:T(2,128)(2,1)}), bf16[256,2,192]{2,1,0:T(2,128)(2,1)S(1)}, u32[]{:S(2)}, u32[]{:S(2)}) async-start(bf16[256,2,192]{2,1,0:T(2,128)(2,1)} %bitcast.8), calls=%async_computation.1 | async-start | bytes 524288 | tf_op jit(solution)/shard_map/all_to_all | solution.py:71
  43.1 14.5 %all-to-all-done.1 = bf16[256,2,192]{2,1,0:T(2,128)(2,1)S(1)} async-done(((bf16[256,2,192]{2,1,0:T(2,128)(2,1)}), bf16[256,2,192]{2,1,0:T(2,128)(2,1)S(1)}, u32[]{:S(2)}, u32[]{:S(2)}) %all-to-all-start.1) | async-done | bytes 196640 | tf_op jit(solution)/shard_map/all_to_all | solution.py:71
  57.6 0.2 reshape.126
  57.8 0.0 copy-done
  57.8 0.3 convolution_multiply_fusion
  58.1 0.8 convolution_convert_fusion
  58.9 0.1 reshape.127
  58.9 16.6 %all_to_all.20 = bf16[64,2,768]{2,1,0:T(2,128)(2,1)S(1)} all-to-all(bf16[64,2,768]{2,1,0:T(2,128)(2,1)S(1)} %reshape.127), channel_id=1, replica_groups=mesh['sector'=64,'dof'=4] {'sector'}, dimensions={0} | all-to-all | bytes 393216 | tf_op jit(solution)/shard_map/all_to_all | solution.py:85
  75.5 0.5 convolution_convert_fusion.2
  75.9 0.2 copy.16
  76.1 16.3 %all_to_all.21 = bf16[64,2,768]{2,1,0:T(2,128)(2,1)S(1)} all-to-all(bf16[64,2,768]{2,1,0:T(2,128)(2,1)S(1)} %copy.16), channel_id=1, replica_groups=mesh['sector'=64,'dof'=4] {'sector'}, dimensions={0} | all-to-all | bytes 393216 | tf_op jit(solution)/shard_map/all_to_all | solution.py:89
  92.4 3.9 %fusion.1 = bf16[1,64,1536]{2,1,0:T(8,128)(2,1)} fusion(bf16[2,768,1536]{2,1,0:T(8,128)(2,1)} %bitcast.97, bf16[64,2,768]{2,1,0:T(2,128)(2,1)S(1)} %all_to_all.21), kind=kOutput, calls=%fused_computation.4 | convolution fusion | flops 302088192 | bytes 5111808 | tf_op jit(solution)/shard_map/thc,hcn->tn/dot_general | solution.py:90
  (16 shorter events, 0.1 us)
Async XLA Ops:
  0.0 57.8 %copy-start = (bf16[1,1536,256]{2,1,0:T(8,128)(2,1)S(1)}, bf16[1,1536,256]{2,1,0:T(8,128)(2,1)}, u32[]{:S(2)}) copy-start(bf16[1,1536,256]{2,1,0:T(8,128)(2,1)} %param.10) | copy-start | bytes 2359300
  0.0 20.1 %copy-start.3 = (s32[64]{0:T(128)S(1)}, s32[64]{0:T(128)}, u32[]{:S(2)}) copy-start(s32[64]{0:T(128)} %param.15) | copy-start | bytes 772
  0.0 20.1 %copy-start.2 = (f32[1,256]{1,0:T(1,128)S(1)}, f32[1,256]{1,0:T(1,128)}, u32[]{:S(2)}) copy-start(f32[1,256]{1,0:T(1,128)} %param.12) | copy-start | bytes 3076
  0.0 20.1 %copy-start.1 = (f32[1,256]{1,0:T(1,128)S(1)}, f32[1,256]{1,0:T(1,128)}, u32[]{:S(2)}) copy-start(f32[1,256]{1,0:T(1,128)} %param.13) | copy-start | bytes 3076
  4.4 30.9 %all-to-all-start = ((bf16[256,2,192]{2,1,0:T(2,128)(2,1)}), bf16[256,2,192]{2,1,0:T(2,128)(2,1)S(1)}, u32[]{:S(2)}, u32[]{:S(2)}) async-start(bf16[256,2,192]{2,1,0:T(2,128)(2,1)} %reshape.123), calls=%async_computation | async-start | bytes 524288 | tf_op jit(solution)/shard_map/all_to_all | solution.py:65
  36.9 20.8 %all-to-all-start.1 = ((bf16[256,2,192]{2,1,0:T(2,128)(2,1)}), bf16[256,2,192]{2,1,0:T(2,128)(2,1)S(1)}, u32[]{:S(2)}, u32[]{:S(2)}) async-start(bf16[256,2,192]{2,1,0:T(2,128)(2,1)} %bitcast.8), calls=%async_computation.1 | async-start | bytes 524288 | tf_op jit(solution)/shard_map/all_to_all | solution.py:71

commit v9 on v8

--- a/solution.py
+++ b/solution.py
@@ -61,16 +61,15 @@
     modes_slot = harmonic_modes[0]
 
     partial_value = jnp.dot(load_history[0], sector_basis, preferred_element_type=jnp.float32)
+    group = ("dof", "sector")
     sent = partial_value.astype(jnp.bfloat16).reshape(n_all, 2, piece // 2)
-    got = lax.all_to_all(sent, ("sector", "dof"), 0, 0, tiled=True).reshape(n_all, piece)
-    wide_table = jnp.repeat(table, n_dof, axis=1)
+    got = lax.all_to_all(sent, group, 0, 0, tiled=True).reshape(n_all, piece)
+    wide_table = jnp.tile(table, (1, n_dof))
     mixed = jnp.dot(wide_table, got.astype(jnp.float32), precision=highest).astype(jnp.bfloat16)
     sent = jnp.broadcast_to(
-        mixed.reshape(n_sector, 1, 2, piece // 2), (n_sector, n_dof, 2, piece // 2)
+        mixed.reshape(1, n_sector, 2, piece // 2), (n_dof, n_sector, 2, piece // 2)
     ).reshape(n_all, 2, piece // 2)
-    spectrum = lax.all_to_all(sent, ("sector", "dof"), 0, 0, tiled=True).reshape(
-        steps_count, reduced_count
-    )
+    spectrum = lax.all_to_all(sent, group, 0, 0, tiled=True).reshape(steps_count, reduced_count)
 
     live = (jnp.arange(modes_slot.shape[1], dtype=jnp.int32) < mode_count[0]).astype(jnp.float32)
     modal = jnp.dot(spectrum, modes_slot, preferred_element_type=jnp.float32) * live[None, :]

time: 96.6 us -> 96.4 us (level)
  no operation moved by 1% of the time
where the time goes in v9:
time: 96.4 us; the launch traced here: 96.1 us
  blocking collectives  32.6 us (34%)
  waiting for transfers between devices  29.4 us (30%)
  starting transfers between devices  20.8 us (22%)
  matrix products  9.12 us (9%)
  local copies, waits for them, and re-layouts  2.85 us (3%)
    all_to_all x1, blocking collectives, local(): lax.all_to_all(returned.reshape(halves), 'sector', 0, 0, tiled=True)  16.3 us
    all_to_all x1, blocking collectives, local(): back = lax.all_to_all(mixed, 'sector', 0, 0, tiled=True)  16.3 us
    all_to_all x1, starting transfers between devices, local(): got = lax.all_to_all(sent, group, 0, 0, tiled=True).reshape(n_all, piece)  15.7 us
    all_to_all x1, waiting for transfers between devices, local(): lax.all_to_all(sent, group, 0, 0, tiled=True)  14.8 us
    all_to_all x1, waiting for transfers between devices, local(): got = lax.all_to_all(sent, group, 0, 0, tiled=True).reshape(n_all, piece)  14.6 us
    all_to_all x1, starting transfers between devices, local(): lax.all_to_all(sent, group, 0, 0, tiled=True)  5.14 us
    dot_general x1, matrix products, local(): jnp.einsum('thc,hcn->tn', back, stress_basis.reshape(halves[1], halves[2]...  3.91 us
    dot_general x1, matrix products, local(): jnp.dot(load_history[0], sector_basis, preferred_element_type=jnp.float32)  3.43 us
  transfers between devices with their start and end apart: 2, of which 2 were waited for; matrix products, arithmetic and copies ran while one was open for 1% of the time, Pallas kernels for 0%

profile of v9, /device:TPU:1, one launch (start us, length us, event | category | flops | bytes accessed | tf_op | source)
XLA Modules:
  0.0 96.1 jit_solution(14099102137368336252)
XLA Ops:
  0.0 3.4 %convolution_convert_fusion.1 = bf16[64,1536]{1,0:T(8,128)(2,1)S(1)} fusion(bf16[1536,1536]{1,0:T(8,128)(2,1)} %param.9, bf16[1,64,1536]{2,1,0:T(8,128)(2,1)} %param.8), kind=kOutput, calls=%fused_computation.3 | convolution fusion | flops 302088192 | bytes 5111808 | tf_op jit(solution)/shard_map/dot_general | solution.py:63
  3.5 1.0 reshape.173
  4.4 15.7 %all-to-all-start = ((bf16[256,2,192]{2,1,0:T(2,128)(2,1)}), bf16[256,2,192]{2,1,0:T(2,128)(2,1)S(1)}, u32[]{:S(2)}, u32[]{:S(2)}) async-start(bf16[256,2,192]{2,1,0:T(2,128)(2,1)} %reshape.173), calls=%async_computation | async-start | bytes 524288 | tf_op jit(solution)/shard_map/all_to_all | solution.py:66
  20.1 0.2 select_multiply_fusion
  20.3 0.1 copy.15
  20.4 0.1 tile.10
  20.5 0.0 copy-done.2
  20.6 0.3 cosine_multiply_fusion
  20.9 14.6 %all-to-all-done = bf16[256,2,192]{2,1,0:T(2,128)(2,1)S(1)} async-done(((bf16[256,2,192]{2,1,0:T(2,128)(2,1)}), bf16[256,2,192]{2,1,0:T(2,128)(2,1)S(1)}, u32[]{:S(2)}, u32[]{:S(2)}) %all-to-all-start) | async-done | bytes 196640 | tf_op jit(solution)/shard_map/all_to_all | solution.py:66
  35.6 0.2 copy.16
  35.8 0.3 convolution_convert_fusion.3
  36.1 0.1 broadcast_in_dim.38
  36.2 0.8 broadcast_in_dim.39
  37.0 5.1 %all-to-all-start.1 = ((bf16[256,2,192]{2,1,0:T(2,128)(2,1)}), bf16[256,2,192]{2,1,0:T(2,128)(2,1)S(1)}, u32[]{:S(2)}, u32[]{:S(2)}) async-start(bf16[256,2,192]{2,1,0:T(2,128)(2,1)} %bitcast.7), calls=%async_computation.1 | async-start | bytes 524288 | tf_op jit(solution)/shard_map/all_to_all | solution.py:72
  42.9 14.8 %all-to-all-done.1 = bf16[256,2,192]{2,1,0:T(2,128)(2,1)S(1)} async-done(((bf16[256,2,192]{2,1,0:T(2,128)(2,1)}), bf16[256,2,192]{2,1,0:T(2,128)(2,1)S(1)}, u32[]{:S(2)}, u32[]{:S(2)}) %all-to-all-start.1) | async-done | bytes 196640 | tf_op jit(solution)/shard_map/all_to_all | solution.py:72
  57.6 0.2 reshape.176
  57.9 0.3 convolution_multiply_fusion
  58.1 0.7 convolution_convert_fusion
  58.9 0.1 reshape.177
  58.9 16.3 %all_to_all.20 = bf16[64,2,768]{2,1,0:T(2,128)(2,1)S(1)} all-to-all(bf16[64,2,768]{2,1,0:T(2,128)(2,1)S(1)} %reshape.177), channel_id=1, replica_groups=mesh['sector'=64,'dof'=4] {'sector'}, dimensions={0} | all-to-all | bytes 393216 | tf_op jit(solution)/shard_map/all_to_all | solution.py:84
  75.2 0.5 convolution_convert_fusion.2
  75.7 0.2 copy.18
  75.9 16.3 %all_to_all.21 = bf16[64,2,768]{2,1,0:T(2,128)(2,1)S(1)} all-to-all(bf16[64,2,768]{2,1,0:T(2,128)(2,1)S(1)} %copy.18), channel_id=1, replica_groups=mesh['sector'=64,'dof'=4] {'sector'}, dimensions={0} | all-to-all | bytes 393216 | tf_op jit(solution)/shard_map/all_to_all | solution.py:88
  92.2 3.9 %fusion.1 = bf16[1,64,1536]{2,1,0:T(8,128)(2,1)} fusion(bf16[2,768,1536]{2,1,0:T(8,128)(2,1)} %bitcast.96, bf16[64,2,768]{2,1,0:T(2,128)(2,1)S(1)} %all_to_all.21), kind=kOutput, calls=%fused_computation.4 | convolution fusion | flops 302088192 | bytes 5111808 | tf_op jit(solution)/shard_map/thc,hcn->tn/dot_general | solution.py:89
  (18 shorter events, 0.1 us)
Async XLA Ops:
  0.0 57.8 %copy-start = (bf16[1,1536,256]{2,1,0:T(8,128)(2,1)S(1)}, bf16[1,1536,256]{2,1,0:T(8,128)(2,1)}, u32[]{:S(2)}) copy-start(bf16[1,1536,256]{2,1,0:T(8,128)(2,1)} %param.10) | copy-start | bytes 2359300
  0.0 20.1 %copy-start.3 = (s32[64]{0:T(128)S(1)}, s32[64]{0:T(128)}, u32[]{:S(2)}) copy-start(s32[64]{0:T(128)} %param.15) | copy-start | bytes 772
  0.0 20.5 %copy-start.2 = (f32[1,256]{1,0:T(1,128)S(1)}, f32[1,256]{1,0:T(1,128)}, u32[]{:S(2)}) copy-start(f32[1,256]{1,0:T(1,128)} %param.12) | copy-start | bytes 3076
  0.0 20.6 %copy-start.1 = (f32[1,256]{1,0:T(1,128)S(1)}, f32[1,256]{1,0:T(1,128)}, u32[]{:S(2)}) copy-start(f32[1,256]{1,0:T(1,128)} %param.13) | copy-start | bytes 3076
  4.4 31.2 %all-to-all-start = ((bf16[256,2,192]{2,1,0:T(2,128)(2,1)}), bf16[256,2,192]{2,1,0:T(2,128)(2,1)S(1)}, u32[]{:S(2)}, u32[]{:S(2)}) async-start(bf16[256,2,192]{2,1,0:T(2,128)(2,1)} %reshape.173), calls=%async_computation | async-start | bytes 524288 | tf_op jit(solution)/shard_map/all_to_all | solution.py:66
  37.0 20.6 %all-to-all-start.1 = ((bf16[256,2,192]{2,1,0:T(2,128)(2,1)}), bf16[256,2,192]{2,1,0:T(2,128)(2,1)S(1)}, u32[]{:S(2)}, u32[]{:S(2)}) async-start(bf16[256,2,192]{2,1,0:T(2,128)(2,1)} %bitcast.7), calls=%async_computation.1 | async-start | bytes 524288 | tf_op jit(solution)/shard_map/all_to_all | solution.py:72

commit v10 on v8

--- a/solution.py
+++ b/solution.py
@@ -61,13 +61,13 @@
     modes_slot = harmonic_modes[0]
 
     partial_value = jnp.dot(load_history[0], sector_basis, preferred_element_type=jnp.float32)
-    sent = partial_value.astype(jnp.bfloat16).reshape(n_all, 2, piece // 2)
+    sent = partial_value.astype(jnp.bfloat16).reshape(n_all, 3, piece // 3)
     got = lax.all_to_all(sent, ("sector", "dof"), 0, 0, tiled=True).reshape(n_all, piece)
     wide_table = jnp.repeat(table, n_dof, axis=1)
     mixed = jnp.dot(wide_table, got.astype(jnp.float32), precision=highest).astype(jnp.bfloat16)
     sent = jnp.broadcast_to(
-        mixed.reshape(n_sector, 1, 2, piece // 2), (n_sector, n_dof, 2, piece // 2)
-    ).reshape(n_all, 2, piece // 2)
+        mixed.reshape(n_sector, 1, 3, piece // 3), (n_sector, n_dof, 3, piece // 3)
+    ).reshape(n_all, 3, piece // 3)
     spectrum = lax.all_to_all(sent, ("sector", "dof"), 0, 0, tiled=True).reshape(
         steps_count, reduced_count
     )

time: 96.6 us -> 96.3 us (level)
  no operation moved by 1% of the time
where the time goes in v10:
time: 96.3 us; the launch traced here: 96 us
  blocking collectives  32.8 us (34%)
  waiting for transfers between devices  29.1 us (30%)
  starting transfers between devices  21.2 us (22%)
  matrix products  9.2 us (10%)
  local copies, waits for them, and re-layouts  2.34 us (2%)
    all_to_all x2, waiting for transfers between devices, local(): lax.all_to_all(sent, ('sector', 'dof'), 0, 0, tiled=True)  29.1 us
    all_to_all x2, starting transfers between devices, local(): lax.all_to_all(sent, ('sector', 'dof'), 0, 0, tiled=True)  21.2 us
    all_to_all x1, blocking collectives, local(): lax.all_to_all(returned.reshape(halves), 'sector', 0, 0, tiled=True)  16.6 us
    all_to_all x1, blocking collectives, local(): back = lax.all_to_all(mixed, 'sector', 0, 0, tiled=True)  16.3 us
    dot_general x1, matrix products, local(): jnp.einsum('thc,hcn->tn', back, stress_basis.reshape(halves[1], halves[2]...  3.91 us
    dot_general x1, matrix products, local(): jnp.dot(load_history[0], sector_basis, preferred_element_type=jnp.float32)  3.43 us
  transfers between devices with their start and end apart: 2, of which 2 were waited for; matrix products, arithmetic and copies ran while one was open for 1% of the time, Pallas kernels for 0%

profile of v10, /device:TPU:1, one launch (start us, length us, event | category | flops | bytes accessed | tf_op | source)
XLA Modules:
  0.0 96.0 jit_solution(437029502445818718)
XLA Ops:
  0.0 0.0 copy-start
  0.0 0.0 copy-start.1
  0.0 3.4 %convolution_convert_fusion.1 = bf16[64,1536]{1,0:T(8,128)(2,1)S(1)} fusion(bf16[1536,1536]{1,0:T(8,128)(2,1)} %param.9, bf16[1,64,1536]{2,1,0:T(8,128)(2,1)} %param.8), kind=kOutput, calls=%fused_computation.3 | convolution fusion | flops 302088192 | bytes 5111808 | tf_op jit(solution)/shard_map/dot_general | solution.py:63
  3.5 0.8 reshape.123
  4.3 15.7 %all-to-all-start = ((bf16[256,3,128]{2,1,0:T(4,128)(2,1)}), bf16[256,3,128]{2,1,0:T(4,128)(2,1)S(1)}, u32[]{:S(2)}, u32[]{:S(2)}) async-start(bf16[256,3,128]{2,1,0:T(4,128)(2,1)} %reshape.123), calls=%async_computation | async-start | bytes 524288 | tf_op jit(solution)/shard_map/all_to_all | solution.py:65
  20.0 0.0 copy-done.3
  20.0 0.0 copy-done.2
  20.1 0.3 cosine_multiply_fusion
  20.4 0.2 select_multiply_fusion
  20.6 14.6 %all-to-all-done = bf16[256,3,128]{2,1,0:T(4,128)(2,1)S(1)} async-done(((bf16[256,3,128]{2,1,0:T(4,128)(2,1)}), bf16[256,3,128]{2,1,0:T(4,128)(2,1)S(1)}, u32[]{:S(2)}, u32[]{:S(2)}) %all-to-all-start) | async-done | bytes 196640 | tf_op jit(solution)/shard_map/all_to_all | solution.py:65
  35.2 0.2 copy.14
  35.4 0.4 convolution_convert_fusion.3
  35.8 0.8 broadcast_in_dim.43
  36.6 5.5 %all-to-all-start.1 = ((bf16[256,3,128]{2,1,0:T(4,128)(2,1)}), bf16[256,3,128]{2,1,0:T(4,128)(2,1)S(1)}, u32[]{:S(2)}, u32[]{:S(2)}) async-start(bf16[256,3,128]{2,1,0:T(4,128)(2,1)} %bitcast.8), calls=%async_computation.1 | async-start | bytes 524288 | tf_op jit(solution)/shard_map/all_to_all | solution.py:71
  42.8 14.5 %all-to-all-done.1 = bf16[256,3,128]{2,1,0:T(4,128)(2,1)S(1)} async-done(((bf16[256,3,128]{2,1,0:T(4,128)(2,1)}), bf16[256,3,128]{2,1,0:T(4,128)(2,1)S(1)}, u32[]{:S(2)}, u32[]{:S(2)}) %all-to-all-start.1) | async-done | bytes 196640 | tf_op jit(solution)/shard_map/all_to_all | solution.py:71
  57.3 0.2 reshape.126
  57.5 0.3 convolution_multiply_fusion
  57.8 0.8 convolution_convert_fusion
  58.6 0.1 reshape.127
  58.6 16.6 %all_to_all.20 = bf16[64,2,768]{2,1,0:T(2,128)(2,1)S(1)} all-to-all(bf16[64,2,768]{2,1,0:T(2,128)(2,1)S(1)} %reshape.127), channel_id=1, replica_groups=mesh['sector'=64,'dof'=4] {'sector'}, dimensions={0} | all-to-all | bytes 393216 | tf_op jit(solution)/shard_map/all_to_all | solution.py:85
  75.2 0.5 convolution_convert_fusion.2
  75.6 0.2 copy.16
  75.8 16.3 %all_to_all.21 = bf16[64,2,768]{2,1,0:T(2,128)(2,1)S(1)} all-to-all(bf16[64,2,768]{2,1,0:T(2,128)(2,1)S(1)} %copy.16), channel_id=1, replica_groups=mesh['sector'=64,'dof'=4] {'sector'}, dimensions={0} | all-to-all | bytes 393216 | tf_op jit(solution)/shard_map/all_to_all | solution.py:89
  92.1 3.9 %fusion.1 = bf16[1,64,1536]{2,1,0:T(8,128)(2,1)} fusion(bf16[2,768,1536]{2,1,0:T(8,128)(2,1)} %bitcast.97, bf16[64,2,768]{2,1,0:T(2,128)(2,1)S(1)} %all_to_all.21), kind=kOutput, calls=%fused_computation.4 | convolution fusion | flops 302088192 | bytes 5111808 | tf_op jit(solution)/shard_map/thc,hcn->tn/dot_general | solution.py:90
  (16 shorter events, 0.2 us)
Async XLA Ops:
  0.0 57.5 %copy-start = (bf16[1,1536,256]{2,1,0:T(8,128)(2,1)S(1)}, bf16[1,1536,256]{2,1,0:T(8,128)(2,1)}, u32[]{:S(2)}) copy-start(bf16[1,1536,256]{2,1,0:T(8,128)(2,1)} %param.10) | copy-start | bytes 2359300
  0.0 20.0 %copy-start.3 = (s32[64]{0:T(128)S(1)}, s32[64]{0:T(128)}, u32[]{:S(2)}) copy-start(s32[64]{0:T(128)} %param.15) | copy-start | bytes 772
  0.0 20.0 %copy-start.2 = (f32[1,256]{1,0:T(1,128)S(1)}, f32[1,256]{1,0:T(1,128)}, u32[]{:S(2)}) copy-start(f32[1,256]{1,0:T(1,128)} %param.12) | copy-start | bytes 3076
  0.0 20.0 %copy-start.1 = (f32[1,256]{1,0:T(1,128)S(1)}, f32[1,256]{1,0:T(1,128)}, u32[]{:S(2)}) copy-start(f32[1,256]{1,0:T(1,128)} %param.13) | copy-start | bytes 3076
  4.3 30.9 %all-to-all-start = ((bf16[256,3,128]{2,1,0:T(4,128)(2,1)}), bf16[256,3,128]{2,1,0:T(4,128)(2,1)S(1)}, u32[]{:S(2)}, u32[]{:S(2)}) async-start(bf16[256,3,128]{2,1,0:T(4,128)(2,1)} %reshape.123), calls=%async_computation | async-start | bytes 524288 | tf_op jit(solution)/shard_map/all_to_all | solution.py:65
  36.6 20.8 %all-to-all-start.1 = ((bf16[256,3,128]{2,1,0:T(4,128)(2,1)}), bf16[256,3,128]{2,1,0:T(4,128)(2,1)S(1)}, u32[]{:S(2)}, u32[]{:S(2)}) async-start(bf16[256,3,128]{2,1,0:T(4,128)(2,1)} %bitcast.8), calls=%async_computation.1 | async-start | bytes 524288 | tf_op jit(solution)/shard_map/all_to_all | solution.py:71

commit v11 on v8

--- a/solution.py
+++ b/solution.py
@@ -83,14 +83,16 @@
     returned = product.astype(jnp.bfloat16)
     halves = (n_sector, 2, reduced_count // 2)
     by_step = lax.all_to_all(returned.reshape(halves), "sector", 0, 0, tiled=True)
-    mixed = jnp.einsum(
+    back = jnp.einsum(
         "js,jhc->shc", table, by_step.astype(jnp.float32), precision=highest
     ).astype(jnp.bfloat16)
-    back = lax.all_to_all(mixed, "sector", 0, 0, tiled=True)
-    stress_field = jnp.einsum(
-        "thc,hcn->tn", back, stress_basis.reshape(halves[1], halves[2], -1),
+    at_step = jnp.einsum(
+        "shc,hcn->sn", back, stress_basis.reshape(halves[1], halves[2], -1),
         preferred_element_type=jnp.float32,
     ).astype(jnp.bfloat16)
+    stress_field = lax.all_to_all(
+        at_step.reshape(n_sector, 2, -1), "sector", 0, 0, tiled=True
+    ).reshape(steps_count, -1)
     return stress_field[None]
 
 

time: 96.6 us -> 96.6 us (level)
  no operation moved by 1% of the time
where the time goes in v11:
time: 96.6 us; the launch traced here: 96.4 us
  blocking collectives  32.9 us (34%)
  waiting for transfers between devices  29.1 us (30%)
  starting transfers between devices  21.2 us (22%)
  matrix products  8.55 us (9%)
  local copies, waits for them, and re-layouts  3.28 us (3%)
    all_to_all x2, waiting for transfers between devices, local(): lax.all_to_all(sent, ('sector', 'dof'), 0, 0, tiled=True)  29.1 us
    all_to_all x2, starting transfers between devices, local(): lax.all_to_all(sent, ('sector', 'dof'), 0, 0, tiled=True)  21.2 us
    all_to_all x1, blocking collectives, local(): lax.all_to_all(returned.reshape(halves), 'sector', 0, 0, tiled=True)  16.6 us
    all_to_all x1, blocking collectives, local(): lax.all_to_all(at_step.reshape(n_sector, 2, -1), 'sector', 0, 0, tiled=True)  16.3 us
    dot_general x1, matrix products, local(): jnp.dot(load_history[0], sector_basis, preferred_element_type=jnp.float32)  3.43 us
    dot_general x1, matrix products, local(): jnp.einsum('shc,hcn->sn', back, stress_basis.reshape(halves[1], halves[2]...  3.26 us
  transfers between devices with their start and end apart: 2, of which 2 were waited for; matrix products, arithmetic and copies ran while one was open for 1% of the time, Pallas kernels for 0%

profile of v11, /device:TPU:1, one launch (start us, length us, event | category | flops | bytes accessed | tf_op | source)
XLA Modules:
  0.0 96.4 jit_solution(10158021672536913716)
XLA Ops:
  0.0 0.0 copy-start
  0.0 0.0 copy-start.1
  0.0 3.4 %convolution_convert_fusion.1 = bf16[64,1536]{1,0:T(8,128)(2,1)S(1)} fusion(bf16[1536,1536]{1,0:T(8,128)(2,1)} %param.9, bf16[1,64,1536]{2,1,0:T(8,128)(2,1)} %param.8), kind=kOutput, calls=%fused_computation.3 | convolution fusion | flops 302088192 | bytes 5111808 | tf_op jit(solution)/shard_map/dot_general | solution.py:63
  3.5 1.0 reshape.126
  4.4 15.7 %all-to-all-start = ((bf16[256,2,192]{2,1,0:T(2,128)(2,1)}), bf16[256,2,192]{2,1,0:T(2,128)(2,1)S(1)}, u32[]{:S(2)}, u32[]{:S(2)}) async-start(bf16[256,2,192]{2,1,0:T(2,128)(2,1)} %reshape.126), calls=%async_computation | async-start | bytes 524288 | tf_op jit(solution)/shard_map/all_to_all | solution.py:65
  20.2 0.3 cosine_multiply_fusion
  20.5 0.2 select_multiply_fusion
  20.7 14.6 %all-to-all-done = bf16[256,2,192]{2,1,0:T(2,128)(2,1)S(1)} async-done(((bf16[256,2,192]{2,1,0:T(2,128)(2,1)}), bf16[256,2,192]{2,1,0:T(2,128)(2,1)S(1)}, u32[]{:S(2)}, u32[]{:S(2)}) %all-to-all-start) | async-done | bytes 196640 | tf_op jit(solution)/shard_map/all_to_all | solution.py:65
  35.3 0.2 copy.9
  35.5 0.4 convolution_convert_fusion.3
  35.9 0.1 broadcast_in_dim.39
  36.0 0.8 broadcast_in_dim.40
  36.9 5.5 %all-to-all-start.1 = ((bf16[256,2,192]{2,1,0:T(2,128)(2,1)}), bf16[256,2,192]{2,1,0:T(2,128)(2,1)S(1)}, u32[]{:S(2)}, u32[]{:S(2)}) async-start(bf16[256,2,192]{2,1,0:T(2,128)(2,1)} %bitcast.8), calls=%async_computation.1 | async-start | bytes 524288 | tf_op jit(solution)/shard_map/all_to_all | solution.py:71
  43.1 14.5 %all-to-all-done.1 = bf16[256,2,192]{2,1,0:T(2,128)(2,1)S(1)} async-done(((bf16[256,2,192]{2,1,0:T(2,128)(2,1)}), bf16[256,2,192]{2,1,0:T(2,128)(2,1)S(1)}, u32[]{:S(2)}, u32[]{:S(2)}) %all-to-all-start.1) | async-done | bytes 196640 | tf_op jit(solution)/shard_map/all_to_all | solution.py:71
  57.6 0.2 reshape.129
  57.8 0.3 convolution_multiply_fusion
  58.1 0.8 convolution_convert_fusion
  58.9 0.1 reshape.130
  58.9 16.6 %all_to_all.20 = bf16[64,2,768]{2,1,0:T(2,128)(2,1)S(1)} all-to-all(bf16[64,2,768]{2,1,0:T(2,128)(2,1)S(1)} %reshape.130), channel_id=1, replica_groups=mesh['sector'=64,'dof'=4] {'sector'}, dimensions={0} | all-to-all | bytes 393216 | tf_op jit(solution)/shard_map/all_to_all | solution.py:85
  75.5 0.5 convolution_convert_fusion.2
  75.9 3.3 %fusion = bf16[64,1536]{1,0:T(8,128)(2,1)S(1)} fusion(bf16[64,2,768]{2,0,1:T(8,128)(2,1)S(1)} %convolution_convert_fusion.2, bf16[2,768,1536]{2,1,0:T(8,128)(2,1)} %bitcast.94), kind=kOutput, calls=%fused_computation.1 | convolution fusion | flops 302088192 | bytes 5111808 | tf_op jit(solution)/shard_map/shc,hcn->sn/dot_general | solution.py:89
  79.2 0.1 reshape.132
  79.3 16.3 %all_to_all.21 = bf16[64,2,768]{2,1,0:T(2,128)(2,1)S(1)} all-to-all(bf16[64,2,768]{2,1,0:T(2,128)(2,1)S(1)} %reshape.132), channel_id=1, replica_groups=mesh['sector'=64,'dof'=4] {'sector'}, dimensions={0} | all-to-all | bytes 393216 | tf_op jit(solution)/shard_map/all_to_all | solution.py:93
  95.6 0.8 broadcast_in_dim_reshape.3
  (17 shorter events, 0.1 us)
Async XLA Ops:
  0.0 57.8 %copy-start = (bf16[1,1536,256]{2,1,0:T(8,128)(2,1)S(1)}, bf16[1,1536,256]{2,1,0:T(8,128)(2,1)}, u32[]{:S(2)}) copy-start(bf16[1,1536,256]{2,1,0:T(8,128)(2,1)} %param.10) | copy-start | bytes 2359300
  0.0 20.1 %copy-start.3 = (s32[64]{0:T(128)S(1)}, s32[64]{0:T(128)}, u32[]{:S(2)}) copy-start(s32[64]{0:T(128)} %param.15) | copy-start | bytes 772
  0.0 20.1 %copy-start.2 = (f32[1,256]{1,0:T(1,128)S(1)}, f32[1,256]{1,0:T(1,128)}, u32[]{:S(2)}) copy-start(f32[1,256]{1,0:T(1,128)} %param.12) | copy-start | bytes 3076
  0.0 20.1 %copy-start.1 = (f32[1,256]{1,0:T(1,128)S(1)}, f32[1,256]{1,0:T(1,128)}, u32[]{:S(2)}) copy-start(f32[1,256]{1,0:T(1,128)} %param.13) | copy-start | bytes 3076
  4.4 30.9 %all-to-all-start = ((bf16[256,2,192]{2,1,0:T(2,128)(2,1)}), bf16[256,2,192]{2,1,0:T(2,128)(2,1)S(1)}, u32[]{:S(2)}, u32[]{:S(2)}) async-start(bf16[256,2,192]{2,1,0:T(2,128)(2,1)} %reshape.126), calls=%async_computation | async-start | bytes 524288 | tf_op jit(solution)/shard_map/all_to_all | solution.py:65
  36.9 20.8 %all-to-all-start.1 = ((bf16[256,2,192]{2,1,0:T(2,128)(2,1)}), bf16[256,2,192]{2,1,0:T(2,128)(2,1)S(1)}, u32[]{:S(2)}, u32[]{:S(2)}) async-start(bf16[256,2,192]{2,1,0:T(2,128)(2,1)} %bitcast.8), calls=%async_computation.1 | async-start | bytes 524288 | tf_op jit(solution)/shard_map/all_to_all | solution.py:71

commit v12 on v8

--- a/solution.py
+++ b/solution.py
@@ -64,7 +64,7 @@
     sent = partial_value.astype(jnp.bfloat16).reshape(n_all, 2, piece // 2)
     got = lax.all_to_all(sent, ("sector", "dof"), 0, 0, tiled=True).reshape(n_all, piece)
     wide_table = jnp.repeat(table, n_dof, axis=1)
-    mixed = jnp.dot(wide_table, got.astype(jnp.float32), precision=highest).astype(jnp.bfloat16)
+    mixed = jnp.dot(wide_table, got.astype(jnp.float32), precision=lax.Precision.HIGH).astype(jnp.bfloat16)
     sent = jnp.broadcast_to(
         mixed.reshape(n_sector, 1, 2, piece // 2), (n_sector, n_dof, 2, piece // 2)
     ).reshape(n_all, 2, piece // 2)
@@ -84,7 +84,7 @@
     halves = (n_sector, 2, reduced_count // 2)
     by_step = lax.all_to_all(returned.reshape(halves), "sector", 0, 0, tiled=True)
     mixed = jnp.einsum(
-        "js,jhc->shc", table, by_step.astype(jnp.float32), precision=highest
+        "js,jhc->shc", table, by_step.astype(jnp.float32), precision=lax.Precision.HIGH
     ).astype(jnp.bfloat16)
     back = lax.all_to_all(mixed, "sector", 0, 0, tiled=True)
     stress_field = jnp.einsum(

time: 96.6 us -> 96.5 us (level)
  no operation moved by 1% of the time
where the time goes in v12:
time: 96.5 us; the launch traced here: 96.2 us
  blocking collectives  32.8 us (34%)
  waiting for transfers between devices  29.1 us (30%)
  starting transfers between devices  21.2 us (22%)
  matrix products  9.06 us (9%)
  local copies, waits for them, and re-layouts  2.63 us (3%)
    all_to_all x2, waiting for transfers between devices, local(): lax.all_to_all(sent, ('sector', 'dof'), 0, 0, tiled=True)  29.1 us
    all_to_all x2, starting transfers between devices, local(): lax.all_to_all(sent, ('sector', 'dof'), 0, 0, tiled=True)  21.2 us
    all_to_all x1, blocking collectives, local(): lax.all_to_all(returned.reshape(halves), 'sector', 0, 0, tiled=True)  16.6 us
    all_to_all x1, blocking collectives, local(): back = lax.all_to_all(mixed, 'sector', 0, 0, tiled=True)  16.3 us
    dot_general x1, matrix products, local(): jnp.einsum('thc,hcn->tn', back, stress_basis.reshape(halves[1], halves[2]...  3.91 us
    dot_general x1, matrix products, local(): jnp.dot(load_history[0], sector_basis, preferred_element_type=jnp.float32)  3.43 us
  transfers between devices with their start and end apart: 2, of which 2 were waited for; matrix products, arithmetic and copies ran while one was open for 1% of the time, Pallas kernels for 0%

profile of v12, /device:TPU:1, one launch (start us, length us, event | category | flops | bytes accessed | tf_op | source)
XLA Modules:
  0.0 96.2 jit_solution(5320518273012298340)
XLA Ops:
  0.0 0.0 copy-start
  0.0 0.0 copy-start.1
  0.0 3.4 %convolution_convert_fusion.1 = bf16[64,1536]{1,0:T(8,128)(2,1)S(1)} fusion(bf16[1536,1536]{1,0:T(8,128)(2,1)} %param.9, bf16[1,64,1536]{2,1,0:T(8,128)(2,1)} %param.8), kind=kOutput, calls=%fused_computation.3 | convolution fusion | flops 302088192 | bytes 5111808 | tf_op jit(solution)/shard_map/dot_general | solution.py:63
  3.5 1.0 reshape.123
  4.4 15.7 %all-to-all-start = ((bf16[256,2,192]{2,1,0:T(2,128)(2,1)}), bf16[256,2,192]{2,1,0:T(2,128)(2,1)S(1)}, u32[]{:S(2)}, u32[]{:S(2)}) async-start(bf16[256,2,192]{2,1,0:T(2,128)(2,1)} %reshape.123), calls=%async_computation | async-start | bytes 524288 | tf_op jit(solution)/shard_map/all_to_all | solution.py:65
  20.1 0.0 copy-done.3
  20.2 0.3 cosine_multiply_fusion
  20.5 0.2 select_multiply_fusion
  20.7 14.6 %all-to-all-done = bf16[256,2,192]{2,1,0:T(2,128)(2,1)S(1)} async-done(((bf16[256,2,192]{2,1,0:T(2,128)(2,1)}), bf16[256,2,192]{2,1,0:T(2,128)(2,1)S(1)}, u32[]{:S(2)}, u32[]{:S(2)}) %all-to-all-start) | async-done | bytes 196640 | tf_op jit(solution)/shard_map/all_to_all | solution.py:65
  35.3 0.2 copy.14
  35.5 0.3 convolution_convert_fusion.3
  35.8 0.1 broadcast_in_dim.42
  35.9 0.8 broadcast_in_dim.43
  36.8 5.5 %all-to-all-start.1 = ((bf16[256,2,192]{2,1,0:T(2,128)(2,1)}), bf16[256,2,192]{2,1,0:T(2,128)(2,1)S(1)}, u32[]{:S(2)}, u32[]{:S(2)}) async-start(bf16[256,2,192]{2,1,0:T(2,128)(2,1)} %bitcast.8), calls=%async_computation.1 | async-start | bytes 524288 | tf_op jit(solution)/shard_map/all_to_all | solution.py:71
  43.0 14.5 %all-to-all-done.1 = bf16[256,2,192]{2,1,0:T(2,128)(2,1)S(1)} async-done(((bf16[256,2,192]{2,1,0:T(2,128)(2,1)}), bf16[256,2,192]{2,1,0:T(2,128)(2,1)S(1)}, u32[]{:S(2)}, u32[]{:S(2)}) %all-to-all-start.1) | async-done | bytes 196640 | tf_op jit(solution)/shard_map/all_to_all | solution.py:71
  57.5 0.2 reshape.126
  57.8 0.3 convolution_multiply_fusion
  58.0 0.8 convolution_convert_fusion
  58.8 0.1 reshape.127
  58.8 16.6 %all_to_all.20 = bf16[64,2,768]{2,1,0:T(2,128)(2,1)S(1)} all-to-all(bf16[64,2,768]{2,1,0:T(2,128)(2,1)S(1)} %reshape.127), channel_id=1, replica_groups=mesh['sector'=64,'dof'=4] {'sector'}, dimensions={0} | all-to-all | bytes 393216 | tf_op jit(solution)/shard_map/all_to_all | solution.py:85
  75.4 0.4 convolution_convert_fusion.2
  75.8 0.2 copy.16
  76.0 16.3 %all_to_all.21 = bf16[64,2,768]{2,1,0:T(2,128)(2,1)S(1)} all-to-all(bf16[64,2,768]{2,1,0:T(2,128)(2,1)S(1)} %copy.16), channel_id=1, replica_groups=mesh['sector'=64,'dof'=4] {'sector'}, dimensions={0} | all-to-all | bytes 393216 | tf_op jit(solution)/shard_map/all_to_all | solution.py:89
  92.3 3.9 %fusion.1 = bf16[1,64,1536]{2,1,0:T(8,128)(2,1)} fusion(bf16[2,768,1536]{2,1,0:T(8,128)(2,1)} %bitcast.97, bf16[64,2,768]{2,1,0:T(2,128)(2,1)S(1)} %all_to_all.21), kind=kOutput, calls=%fused_computation.4 | convolution fusion | flops 302088192 | bytes 5111808 | tf_op jit(solution)/shard_map/thc,hcn->tn/dot_general | solution.py:90
  (16 shorter events, 0.1 us)
Async XLA Ops:
  0.0 57.7 %copy-start = (bf16[1,1536,256]{2,1,0:T(8,128)(2,1)S(1)}, bf16[1,1536,256]{2,1,0:T(8,128)(2,1)}, u32[]{:S(2)}) copy-start(bf16[1,1536,256]{2,1,0:T(8,128)(2,1)} %param.10) | copy-start | bytes 2359300
  0.0 20.1 %copy-start.3 = (s32[64]{0:T(128)S(1)}, s32[64]{0:T(128)}, u32[]{:S(2)}) copy-start(s32[64]{0:T(128)} %param.15) | copy-start | bytes 772
  0.0 20.1 %copy-start.2 = (f32[1,256]{1,0:T(1,128)S(1)}, f32[1,256]{1,0:T(1,128)}, u32[]{:S(2)}) copy-start(f32[1,256]{1,0:T(1,128)} %param.12) | copy-start | bytes 3076
  0.0 20.1 %copy-start.1 = (f32[1,256]{1,0:T(1,128)S(1)}, f32[1,256]{1,0:T(1,128)}, u32[]{:S(2)}) copy-start(f32[1,256]{1,0:T(1,128)} %param.13) | copy-start | bytes 3076
  4.4 30.9 %all-to-all-start = ((bf16[256,2,192]{2,1,0:T(2,128)(2,1)}), bf16[256,2,192]{2,1,0:T(2,128)(2,1)S(1)}, u32[]{:S(2)}, u32[]{:S(2)}) async-start(bf16[256,2,192]{2,1,0:T(2,128)(2,1)} %reshape.123), calls=%async_computation | async-start | bytes 524288 | tf_op jit(solution)/shard_map/all_to_all | solution.py:65
  36.8 20.8 %all-to-all-start.1 = ((bf16[256,2,192]{2,1,0:T(2,128)(2,1)}), bf16[256,2,192]{2,1,0:T(2,128)(2,1)S(1)}, u32[]{:S(2)}, u32[]{:S(2)}) async-start(bf16[256,2,192]{2,1,0:T(2,128)(2,1)} %bitcast.8), calls=%async_computation.1 | async-start | bytes 524288 | tf_op jit(solution)/shard_map/all_to_all | solution.py:71
